TPU v7x, 128 devices: a whole 4x4x4 slice. The times are simulated.
128 devices in a mesh: seq: 32 (over x, y_lo, z), tp: 2 (over core), pd: 2 (over y_hi).
Axes of the slice: x: 4, y: 4 (y_hi: 2, y_lo: 2; y = y_hi * 2 + y_lo), z: 4, core: 2. Of those that a mesh axis runs over, the one named last changes fastest.
Arguments:
- hidden_in: bfloat16 [2, 8192, 2048], P('pd', 'seq'), may hold values from -6 to 6
- input_gain: float32 [2048], replicated, may hold values from 0.5 to 1.5
- w_query: bfloat16 [2048, 2048], P(None, 'tp'), may hold values from -0.125 to 0.125
- w_key: bfloat16 [2048, 256], P(None, 'tp'), may hold values from -0.125 to 0.125
- w_value: bfloat16 [2048, 256], P(None, 'tp'), may hold values from -0.125 to 0.125
- q_gain: float32 [128], replicated, may hold values from 0.1 to 1.9
- k_gain: float32 [128], replicated, may hold values from 0.1 to 1.9
- w_out: bfloat16 [2048, 2048], P('tp'), may hold values from -0.125 to 0.125
- post_gain: float32 [2048], replicated, may hold values from 0.5 to 1.5
- ctx_key: bfloat16 [2, 2048, 256], P('pd', 'seq', 'tp'), may hold values from -70 to 70
- ctx_value: bfloat16 [2, 2048, 256], P('pd', 'seq', 'tp'), may hold values from -6 to 6
- span_lens: int32 [2, 8], P('pd'), may hold values from 1 to 4096, 8192 in all within a row
- ctx_lens: int32 [2, 8], P('pd'), may hold values from 1 to 1024, 2048 in all within a row
- route_ids: int32 [2, 8192, 8], P('pd', ('seq', 'tp')), may hold values from 0 to 127, all different within a row; in each aligned block of 128 rows (0 to 127, 128 to 255, ..., all dimensions but the last counted through in order) at most 12 rows name the same one
- route_weights: float32 [2, 8192, 8], P('pd', ('seq', 'tp')), may hold values from 0.05 to 1
- w_gate_up: bfloat16 [128, 2048, 1536], P(('seq', 'tp', 'pd')), may hold values from -0.125 to 0.125
- w_down: bfloat16 [128, 768, 2048], P(('seq', 'tp', 'pd')), may hold values from -0.21875 to 0.21875
- earlier_kv: bfloat16 [8, 2, 8192, 2, 256], P(None, 'pd', 'seq', 'tp'), may hold values from -6 to 6
- page_table: int32 [8, 2, 64, 2], P(None, 'pd', 'seq', 'tp'), may hold values from 0 to 511, as said below
Outputs:
- layer_out: bfloat16 [2, 8192, 2048], P('pd', ('seq', 'tp'))
- decode_cache: bfloat16 [32, 2, 2, 16, 128, 256], P('seq', 'tp', 'pd')
Inputs may be any that keep to these rules, and one draw needn't show every extreme that they name: `route_ids`: within the rows of one device no expert is named more than 12 times, a bound that some block reaches. `page_table`: an entry owner * 16 + slot sends the page to that slot of the device at index owner of seq, with the same indices of tp and pd. Every slot of every owner receives exactly one page; one device sends at most 1 pages to one owner, and exactly that many to some owner.
All inputs are finite; a program needn't handle non-finite values.
Results may differ from a plain program's by a relative error of at most 0.015.
Values may be sent and summed in bfloat16 or wider, within the bound.
No kernel may reach another device: no remote copies, remote signals or barrier semaphores. Data moves between devices by JAX's collectives and lax.ppermute only.
A program may use at most 128 MiB of HBM per device.

v0:
```python
import math

import jax
import jax.numpy as jnp
from jax import lax
from jax.sharding import PartitionSpec as P

PAGE = 128


def rms_norm(values, gain):
    return values * lax.rsqrt(jnp.mean(values * values, axis=-1, keepdims=True) + 1e-06) * gain


def rotate(values, places):
    half = values.shape[-1] // 2
    freq = jnp.exp(
        jnp.arange(half, dtype=jnp.float32) * (-2.0 * math.log(1000000.0) / values.shape[-1])
    )
    angle = places.astype(jnp.float32)[:, None] * freq[None, :]
    cosine = jnp.cos(angle)[:, None, :]
    sine = jnp.sin(angle)[:, None, :]
    first = values[..., :half]
    second = values[..., half:]
    return jnp.concatenate(
        [first * cosine - second * sine, second * cosine + first * sine], axis=-1
    )


def query_places(lengths, context_lengths, places):
    ends = jnp.cumsum(lengths)
    starts = ends - lengths
    request = jnp.sum((places[:, None] >= ends[None, :]).astype(jnp.int32), axis=1)
    member = request[:, None] == jnp.arange(lengths.shape[0], dtype=jnp.int32)[None, :]
    first = jnp.sum(jnp.where(member, starts[None, :], 0), axis=1)
    prior = jnp.sum(jnp.where(member, context_lengths[None, :], 0), axis=1)
    return (request, places - first + prior)


def context_places(context_lengths, places):
    ends = jnp.cumsum(context_lengths)
    starts = ends - context_lengths
    request = jnp.sum((places[:, None] >= ends[None, :]).astype(jnp.int32), axis=1)
    member = request[:, None] == jnp.arange(context_lengths.shape[0], dtype=jnp.int32)[None, :]
    first = jnp.sum(jnp.where(member, starts[None, :], 0), axis=1)
    return (request, places - first)


def expert_mlp(arrived, w_gate_up, w_down):
    hidden = jnp.einsum("sejd,edf->sejf", arrived, w_gate_up, preferred_element_type=jnp.float32)
    inner = hidden.shape[-1] // 2
    act = (jax.nn.silu(hidden[..., :inner]) * hidden[..., inner:]).astype(jnp.bfloat16)
    return jnp.einsum("sejf,efd->sejd", act, w_down, preferred_element_type=jnp.float32).astype(
        jnp.bfloat16
    )


def shards(
    hidden_in,
    input_gain,
    w_query,
    w_key,
    w_value,
    q_gain,
    k_gain,
    w_out,
    post_gain,
    ctx_key,
    ctx_value,
    span_lens,
    ctx_lens,
    route_ids,
    route_weights,
    w_gate_up,
    w_down,
    earlier_kv,
    page_table,
):
    tokens = hidden_in[0]
    tok_count = tokens.shape[0]
    width = tokens.shape[1]
    ctx_count = ctx_key.shape[1]
    head_dim = q_gain.shape[0]
    seq_index = lax.axis_index("seq")
    span_places = seq_index * tok_count + jnp.arange(tok_count, dtype=jnp.int32)
    ctx_index = seq_index * ctx_count + jnp.arange(ctx_count, dtype=jnp.int32)
    query_req, query_pos = query_places(span_lens[0], ctx_lens[0], span_places)
    ctx_req, ctx_pos = context_places(ctx_lens[0], ctx_index)
    normed = rms_norm(tokens.astype(jnp.float32), input_gain).astype(jnp.bfloat16)
    query = jnp.dot(normed, w_query, preferred_element_type=jnp.float32)
    key_proj = jnp.dot(normed, w_key, preferred_element_type=jnp.float32)
    value_proj = jnp.dot(normed, w_value, preferred_element_type=jnp.float32).astype(jnp.bfloat16)
    query_heads = w_query.shape[1] // head_dim
    kv_local = w_key.shape[1] // head_dim
    group = query_heads // kv_local
    queries = rotate(
        rms_norm(query.reshape(tok_count, query_heads, head_dim), q_gain), query_pos
    ).astype(jnp.bfloat16)
    queries = queries.reshape(tok_count, kv_local, group, head_dim).transpose(1, 2, 0, 3)
    span_keys = rotate(
        rms_norm(key_proj.reshape(tok_count, kv_local, head_dim), k_gain), query_pos
    ).astype(jnp.bfloat16)
    all_keys = jnp.concatenate(
        [ctx_key[0], span_keys.reshape(tok_count, kv_local * head_dim)], axis=0
    )
    all_values = jnp.concatenate([ctx_value[0], value_proj], axis=0)
    key_req = jnp.concatenate([ctx_req, query_req], axis=0)
    key_pos = jnp.concatenate([ctx_pos, query_pos], axis=0)
    scale = 1.0 / math.sqrt(head_dim)
    start_state = (
        jnp.full((kv_local, group, tok_count), -1e30, jnp.float32),
        jnp.zeros((kv_local, group, tok_count), jnp.float32),
        jnp.zeros((kv_local, group, tok_count, head_dim), jnp.float32),
    )
    state = start_state
    piece_keys = lax.all_gather(all_keys, "seq", axis=0, tiled=True)
    piece_values = lax.all_gather(all_values, "seq", axis=0, tiled=True)
    piece_req = lax.all_gather(key_req, "seq", axis=0, tiled=True)
    piece_pos = lax.all_gather(key_pos, "seq", axis=0, tiled=True)
    length = piece_keys.shape[0]
    block = length
    for candidate in (2048, 1280, 1024, 640, 512):
        block = candidate
        break
    count = length // block

    def advance(running, items):
        block_keys, block_values, block_req, block_pos = items
        key_heads = block_keys.reshape(block, kv_local, head_dim)
        value_heads = block_values.reshape(block, kv_local, head_dim)
        visible = (query_req[:, None] == block_req[None, :]) & (
            block_pos[None, :] <= query_pos[:, None]
        )
        largest, total, accum = running
        scores = (
            jnp.einsum("hgtd,khd->hgtk", queries, key_heads, preferred_element_type=jnp.float32)
            * scale
        )
        scores = jnp.where(visible[None, None], scores, -jnp.inf)
        new_largest = jnp.maximum(largest, jnp.max(scores, axis=-1))
        expo = jnp.exp(scores - new_largest[..., None])
        factor = jnp.exp(largest - new_largest)
        total = factor * total + jnp.sum(expo, axis=-1)
        accum = factor[..., None] * accum + jnp.einsum(
            "hgtk,khd->hgtd",
            expo.astype(jnp.bfloat16),
            value_heads,
            preferred_element_type=jnp.float32,
        )
        running = (new_largest, total, accum)
        return (running, None)

    stacked = (
        piece_keys.reshape(count, block, -1),
        piece_values.reshape(count, block, -1),
        piece_req.reshape(count, block),
        piece_pos.reshape(count, block),
    )
    state, _ = lax.scan(advance, state, stacked)
    largest, total, accum = state
    attn = (
        (accum / total[..., None])
        .transpose(2, 0, 1, 3)
        .reshape(tok_count, query_heads * head_dim)
        .astype(jnp.bfloat16)
    )
    half = tok_count // lax.axis_size("tp")
    proj = lax.psum_scatter(
        jnp.dot(attn, w_out, preferred_element_type=jnp.float32).astype(jnp.bfloat16),
        "tp",
        scatter_dimension=0,
        tiled=True,
    ).astype(jnp.float32)
    own_rows = lax.dynamic_slice_in_dim(tokens, lax.axis_index("tp") * half, half, 0)
    resid = (own_rows.astype(jnp.float32) + proj).astype(jnp.bfloat16)
    mixed = rms_norm(resid.astype(jnp.float32), post_gain).astype(jnp.bfloat16)
    top = route_ids.shape[2]
    row_ids = route_ids[0].reshape(-1)
    row_count = row_ids.shape[0]
    seq_tp = lax.axis_size("seq") * lax.axis_size("tp")
    pd_count = lax.axis_size("pd")
    device_count = seq_tp * pd_count
    exp_local = w_gate_up.shape[0]
    experts = device_count * exp_local
    capacity = max(2, 3 * tok_count * top // (2 * lax.axis_size("tp") * experts))
    picks = (row_ids[:, None] == jnp.arange(experts, dtype=jnp.int32)[None, :]).astype(jnp.bfloat16)
    earlier = (
        lax.broadcasted_iota(jnp.int32, (row_count, row_count), 0)
        > lax.broadcasted_iota(jnp.int32, (row_count, row_count), 1)
    ).astype(jnp.bfloat16)
    before = jnp.dot(earlier, picks, preferred_element_type=jnp.float32)
    rank = jnp.sum(before * picks.astype(jnp.float32), axis=1).astype(jnp.int32)
    target = row_ids * capacity + rank
    row_token = jnp.arange(row_count, dtype=jnp.int32) // top
    outgoing = jnp.zeros((experts * capacity, width), jnp.bfloat16).at[target].set(mixed[row_token])
    outgoing = outgoing.reshape(device_count, exp_local, capacity, width)
    returned = lax.all_to_all(
        expert_mlp(
            lax.all_to_all(outgoing, ("seq", "tp", "pd"), split_axis=0, concat_axis=0, tiled=True),
            w_gate_up,
            w_down,
        ),
        ("seq", "tp", "pd"),
        split_axis=0,
        concat_axis=0,
        tiled=True,
    )
    gathered = returned.reshape(experts * capacity, width)[target]
    weights = route_weights[0]
    weights = weights / jnp.sum(weights, axis=-1, keepdims=True)
    moe = jnp.einsum(
        "tkd,tk->td",
        gathered.reshape(half, top, width),
        weights,
        preferred_element_type=jnp.float32,
    )
    layer_out = (resid.astype(jnp.float32) + moe).astype(jnp.bfloat16)[None]
    layers = earlier_kv.shape[0]
    per_device = tok_count // PAGE
    page_count = layers * per_device
    seq_size = lax.axis_size("seq")
    page_cap = max(1, page_count // seq_size)
    pages = earlier_kv[:, 0].reshape(layers, per_device, PAGE, kv_local, 2 * head_dim)
    pages = pages.transpose(3, 0, 1, 2, 4).reshape(kv_local, page_count, PAGE, 2 * head_dim)
    table = page_table[:, 0].transpose(2, 0, 1).reshape(kv_local, page_count)
    owners = table // page_count
    slots = table % page_count
    order = jnp.arange(page_count, dtype=jnp.int32)
    same = (owners[:, :, None] == owners[:, None, :]) & (
        order[None, None, :] < order[None, :, None]
    )
    page_rank = jnp.sum(same.astype(jnp.int32), axis=2)
    page_target = owners * page_cap + page_rank
    head_rows = jnp.broadcast_to(jnp.arange(kv_local, dtype=jnp.int32)[:, None], page_target.shape)
    outgoing_pages = (
        jnp.zeros((kv_local, seq_size * page_cap, PAGE, 2 * head_dim), jnp.bfloat16)
        .at[head_rows, page_target]
        .set(pages)
    )
    outgoing_slots = (
        jnp.full((kv_local, seq_size * page_cap), -1, jnp.int32)
        .at[head_rows, page_target]
        .set(slots)
    )
    arrived_pages, arrived_slots = (
        lax.all_to_all(outgoing_pages, "seq", split_axis=1, concat_axis=1, tiled=True),
        lax.all_to_all(outgoing_slots, "seq", split_axis=1, concat_axis=1, tiled=True),
    )
    placing = (arrived_slots[:, None, :] == order[None, :, None]).astype(jnp.bfloat16)
    cache = jnp.einsum(
        "hkr,hrpc->hkpc", placing, arrived_pages, preferred_element_type=jnp.float32
    ).astype(jnp.bfloat16)
    decode_cache = cache[None, :, None]
    return (layer_out, decode_cache)


def solution(mesh):
    in_specs = (
        P("pd", "seq", None),
        P(),
        P(None, "tp"),
        P(None, "tp"),
        P(None, "tp"),
        P(),
        P(),
        P("tp", None),
        P(),
        P("pd", "seq", "tp"),
        P("pd", "seq", "tp"),
        P("pd", None),
        P("pd", None),
        P("pd", ("seq", "tp"), None),
        P("pd", ("seq", "tp"), None),
        P(("seq", "tp", "pd"), None, None),
        P(("seq", "tp", "pd"), None, None),
        P(None, "pd", "seq", "tp", None),
        P(None, "pd", "seq", "tp"),
    )
    out_specs = (P("pd", ("seq", "tp"), None), P("seq", "tp", "pd", None, None, None))
    return jax.shard_map(shards, mesh=mesh, in_specs=in_specs, out_specs=out_specs, check_vma=False)
```

profile of v0, /device:TPU:25, one launch (start us, length us, event | category | flops | bytes accessed | tf_op | source)
XLA Modules:
  0.0 1119.1 jit_solution(3594763674673862545)
XLA Ops:
  14.4 1.5 fusion.44
  15.9 2.0 multiply_reduce_fusion.1
  20.8 1.9 convolution_convert_fusion.1
  23.9 6.5 copy.102
  30.4 3.9 multiply_reduce_fusion
  35.8 2.1 copy.85
  37.9 237.3 %all-reduce.6.cloned.1.call-done = (s32[10240]{0:T(1024)}, s32[10240]{0:T(1024)}) async-done(((s32[10240]{0:T(1024)}, s32[10240]{0:T(1024)}), (s32[10240]{0:T(1024)}, s32[10240]{0:T(1024)})) %all-reduce.6.cloned.1.call-update) | async-done | bytes 81936
  276.8 141.6 %all-gather.3.cloned.1.call-done = bf16[10240,128]{1,0:T(8,128)(2,1)} async-done(((bf16[320,128]{1,0:T(8,128)(2,1)}), bf16[10240,128]{1,0:T(8,128)(2,1)}) %all-gather.3.cloned.1.call-update) | async-done | bytes 2621456 | tf_op jit(solution)/shard_map/all_gather | solution.py:116
  418.4 155.4 %all-gather.5.cloned.1.call-done = bf16[10240,128]{1,0:T(8,128)(2,1)} async-done(((bf16[320,128]{1,0:T(8,128)(2,1)}), bf16[10240,128]{1,0:T(8,128)(2,1)}) %all-gather.5.cloned.1.call-update) | async-done | bytes 2621456 | tf_op jit(solution)/shard_map/all_gather | solution.py:117
  573.8 147.5 %while.15 = (s32[]{:T(128)}, f32[1,8,256]{2,1,0:T(8,128)S(1)}, f32[1,8,256]{2,1,0:T(8,128)S(1)}, f32[1,8,256,128]{3,2,1,0:T(8,128)}, s32[256]{0:T(256)S(1)}, /*i...) while((s32[]{:T(128)}, f32[1,8,256]{2,1,0:T(8,128)S(1)}, ...), condition=%wide.region_13.14_spmd.clone, body=%wide.region_10.13_spmd.clone.sunk | while | flops 2195992576 | bytes 58379428 | solution.py:159
  575.3 9.6 fusion.118
  584.9 9.0 fusion.121
  593.9 9.2 fusion.120
  603.1 1.4 compare_and_fusion.2
  604.6 9.6 fusion.118
  614.2 9.2 fusion.121
  623.4 9.2 fusion.120
  632.7 1.4 compare_and_fusion.2
  634.1 9.6 fusion.118
  643.7 9.2 fusion.121
  653.0 9.2 fusion.120
  663.7 9.6 fusion.118
  673.3 9.2 fusion.121
  682.5 9.2 fusion.120
  693.2 9.6 fusion.118
  702.8 9.2 fusion.121
  712.0 9.2 fusion.120
  721.3 2.6 copy.86
  725.2 4.4 convolution_convert_fusion
  731.6 13.0 %all-to-all-start.2 = ((s32[1,32,1]{2,0,1:T(1,128)}), s32[1,32,1]{2,0,1:T(1,128)S(1)}, u32[]{:S(2)}, u32[]{:S(2)}) async-start(s32[1,32,1]{2,0,1:T(1,128)} %copy.95), calls=%async_computation.3 | async-start | bytes 32768 | tf_op jit(solution)/shard_map/all_to_all | solution.py:247
  745.7 23.6 %reduce-scatter.2.cloned.1.call-done = bf16[128,2048]{1,0:T(8,128)(2,1)} async-done(((bf16[256,2048]{1,0:T(8,128)(2,1)}), bf16[128,2048]{1,0:T(8,128)(2,1)}) %reduce-scatter.2.cloned.1.call-update) | async-done | bytes 524304 | tf_op jit(solution)/shard_map/reduce_scatter | solution.py:168
  769.2 1.5 fusion.60
  772.5 23.8 %scatter_custom_fusion = bf16[1536,2048]{1,0:T(8,128)(2,1)} fusion(s32[1024]{0:T(1024)S(1)} %bitcast.240, bf16[128,2048]{1,0:T(8,128)(2,1)} %fusion.62, s32[1024]{0:T(1024)S(1)} %broadcast_clamp_fusion.1, bf16[]{:T(256)} %constant.110.clone.1), kind=kCustom, calls=%fused_computation.43 | custom fusion | bytes 6291968 | tf_op jit(solution)/shard_map/scatter | solution.py:195
  796.3 10.6 reshape.822
  806.9 9.8 all-to-all-start
  816.7 1.5 broadcast.551
  818.2 3.4 scatter_fusion
  821.6 104.7 %all-to-all-done = bf16[128,1,12,2048]{3,2,1,0:T(8,128)(2,1)} async-done(((bf16[128,1,12,2048]{3,2,1,0:T(8,128)(2,1)}), bf16[128,1,12,2048]{3,2,1,0:T(8,128)(2,1)}, u32[]{:S(2)}, u32[]{:S(2)}) %all-to-all-start) | async-done | bytes 6291488 | tf_op jit(solution)/shard_map/all_to_all | solution.py:199
  926.3 9.0 all-to-all-start.3
  935.4 16.7 %fusion.27 = f32[128,1,12,1536]{3,0,2,1:T(8,128)S(1)} fusion(bf16[1,2048,1536]{2,1,0:T(8,128)(2,1)} %param.36, bf16[128,1,12,2048]{3,2,1,0:T(8,128)(2,1)} %all-to-all-done), kind=kOutput, calls=%fused_computation.38 | convolution fusion | flops 9663676416 | bytes 22020096 | tf_op jit(solution)/shard_map/sejd,edf->sejf/dot_general | solution.py:50
  952.1 5.4 convert_bitcast_fusion
  957.5 6.8 copy.91
  964.3 10.6 all-to-all-start.1
  975.8 2.8 fusion.55
  980.0 104.6 %all-to-all-done.1 = bf16[128,1,12,2048]{3,2,1,0:T(8,128)(2,1)} async-done(((bf16[128,1,12,2048]{3,2,1,0:T(8,128)(2,1)}), bf16[128,1,12,2048]{3,2,1,0:T(8,128)(2,1)}, u32[]{:S(2)}, u32[]{:S(2)}) %all-to-all-start.1) | async-done | bytes 6291488 | tf_op jit(solution)/shard_map/all_to_all | solution.py:197
  1084.6 10.7 reshape.827
  1095.3 12.4 %gather_fusion = bf16[1024,2048]{1,0:T(8,128)(2,1)} fusion(bf16[1536,2048]{1,0:T(8,128)(2,1)} %reshape.827, s32[1024]{0:T(1024)S(1)} %broadcast_clamp_fusion), kind=kCustom, calls=%fused_computation.1 | custom fusion | bytes 8392704 | tf_op jit(solution)/shard_map/gather | solution.py:208
  1107.7 3.5 fusion.33
  (135 shorter events, 27.5 us)
Async XLA Ops:
  7.2 945.0 %copy-start = (bf16[1,768,2048]{2,1,0:T(8,128)(2,1)S(1)}, bf16[1,768,2048]{2,1,0:T(8,128)(2,1)}, u32[]{:S(2)}) copy-start(bf16[1,768,2048]{2,1,0:T(8,128)(2,1)} %param.37) | copy-start | bytes 9437188
  7.2 13.6 %copy-start.12 = (f32[2048]{0:T(1024)S(1)}, f32[2048]{0:T(1024)}, u32[]{:S(2)}) copy-start(f32[2048]{0:T(1024)} %param.22) | copy-start | bytes 24580
  7.2 15.4 %copy-start.6 = (bf16[1,64,128]{2,1,0:T(8,128)(2,1)S(1)}, bf16[1,64,128]{2,1,0:T(8,128)(2,1)}, u32[]{:S(2)}) copy-start(bf16[1,64,128]{2,1,0:T(8,128)(2,1)} %param.31) | copy-start | bytes 49156
  7.2 268.0 %all-reduce.6.cloned.1.call-start = ((), (), s32[]{:S(2)}) async-start(), calls=%async_computation.8 | async-start | bytes 163840
  13.5 0.6 copy-start.5
  13.7 0.6 copy-start.4
  14.4 404.0 %all-gather.3.cloned.1.call-start = ((), (), s32[]{:S(2)}) async-start(), calls=%async_computation.5 | async-start | bytes 2703360 | tf_op jit(solution)/shard_map/all_gather | solution.py:116
  20.7 553.1 %all-gather.5.cloned.1.call-start = ((), (), s32[]{:S(2)}) async-start(), calls=%async_computation.6 | async-start | bytes 2703360 | tf_op jit(solution)/shard_map/all_gather | solution.py:117
  23.3 745.9 %reduce-scatter.2.cloned.1.call-start = ((), (), s32[]{:S(2)}) async-start(), calls=%async_computation.7 | async-start | bytes 1572864 | tf_op jit(solution)/shard_map/reduce_scatter | solution.py:168
  30.4 4.3 copy-start.11
  575.3 9.6 copy-start.1
  604.6 9.6 copy-start.1
  634.1 9.6 copy-start.1
  663.7 9.6 copy-start.1
  693.2 9.6 copy-start.1
  725.2 4.5 copy-start.10
  725.2 19.4 %copy-start.7 = (s32[1,128,8]{1,2,0:T(8,128)S(1)}, s32[1,128,8]{1,2,0:T(8,128)}, u32[]{:S(2)}) copy-start(s32[1,128,8]{1,2,0:T(8,128)} %param.34) | copy-start | bytes 12292
  729.6 41.9 %copy-start.9 = (f32[2048]{0:T(1024)S(1)}, f32[2048]{0:T(1024)}, u32[]{:S(2)}) copy-start(f32[2048]{0:T(1024)} %param.29) | copy-start | bytes 24580
  731.6 75.3 %all-to-all-start.2 = ((s32[1,32,1]{2,0,1:T(1,128)}), s32[1,32,1]{2,0,1:T(1,128)S(1)}, u32[]{:S(2)}, u32[]{:S(2)}) async-start(s32[1,32,1]{2,0,1:T(1,128)} %copy.95), calls=%async_computation.3 | async-start | bytes 32768 | tf_op jit(solution)/shard_map/all_to_all | solution.py:247
  770.7 0.8 copy-start.2
  806.9 119.4 %all-to-all-start = ((bf16[128,1,12,2048]{3,2,1,0:T(8,128)(2,1)}), bf16[128,1,12,2048]{3,2,1,0:T(8,128)(2,1)}, u32[]{:S(2)}, u32[]{:S(2)}) async-start(bf16[128,1,12,2048]{3,2,1,0:T(8,128)(2,1)} %bitcast.226), calls=%async_computation.1 | async-start | bytes 16777216 | tf_op jit(solution)/shard_map/all_to_all | solution.py:199
  926.3 38.0 %all-to-all-start.3 = ((bf16[1,32,128,256]{3,2,0,1:T(8,128)(2,1)}), bf16[1,32,128,256]{3,2,0,1:T(8,128)(2,1)}, u32[]{:S(2)}, u32[]{:S(2)}) async-start(bf16[1,32,128,256]{3,2,0,1:T(8,128)(2,1)} %bitcast.227), calls=%async_computation.4 | async-start | bytes 4194304 | tf_op jit(solution)/shard_map/all_to_all | solution.py:246
  964.3 10.6 copy-start.8
  964.3 120.2 %all-to-all-start.1 = ((bf16[128,1,12,2048]{3,2,1,0:T(8,128)(2,1)}), bf16[128,1,12,2048]{3,2,1,0:T(8,128)(2,1)}, u32[]{:S(2)}, u32[]{:S(2)}) async-start(bf16[128,1,12,2048]{3,2,1,0:T(8,128)(2,1)} %copy.91), calls=%async_computation.2 | async-start | bytes 16777216 | tf_op jit(solution)/shard_map/all_to_all | solution.py:197
  1107.7 3.5 copy-start.3
Sparse Core Ops, SparseCore 0:
  14.5 260.6 all-reduce.5
  276.8 141.4 all-gather.2
  420.0 153.7 all-gather.4
  729.8 39.4 reduce-scatter.1
where the time goes:
time: 1130 us; the launch traced here: 1120 us
  waiting for transfers between devices  767 us (68%)
  matrix products  135 us (12%)
  local copies, waits for them, and re-layouts  89.9 us (8%)
  other arithmetic  68.6 us (6%)
  starting transfers between devices  43.1 us (4%)
  between operations  15.1 us (1%)
    unnamed x5, waiting for transfers between devices  237 us
    all_gather x1, waiting for transfers between devices, shards(): piece_values = lax.all_gather(all_values, 'seq', axis=0, tiled=True)  155 us
    all_gather x1, waiting for transfers between devices, shards(): piece_keys = lax.all_gather(all_keys, 'seq', axis=0, tiled=True)  142 us
    all_to_all x1, waiting for transfers between devices, shards(): lax.all_to_all(outgoing, ('seq', 'tp', 'pd'), split_axis=0, concat_axis=0...  105 us
    all_to_all x1, waiting for transfers between devices, shards(): lax.all_to_all(expert_mlp(lax.all_to_all(outgoing, ('seq', 'tp', 'pd'), s...  105 us
    dot_general x5, matrix products, advance(): jnp.einsum('hgtd,khd->hgtk', queries, key_heads, preferred_element_type=j...  47.9 us
    reduce_sum x5, other arithmetic, advance(): total = factor * total + jnp.sum(expo, axis=-1)  46 us
    dot_general x5, matrix products, advance(): jnp.einsum('hgtk,khd->hgtd', expo.astype(jnp.bfloat16), value_heads, pref...  45.8 us
  transfers between devices with their start and end apart: 8, of which 6 were waited for; matrix products, arithmetic and copies ran while one was open for 9% of the time, Pallas kernels for 0%

commit v1 on v0

--- a/solution.py
+++ b/solution.py
@@ -104,8 +104,21 @@
         [ctx_key[0], span_keys.reshape(tok_count, kv_local * head_dim)], axis=0
     )
     all_values = jnp.concatenate([ctx_value[0], value_proj], axis=0)
-    key_req = jnp.concatenate([ctx_req, query_req], axis=0)
-    key_pos = jnp.concatenate([ctx_pos, query_pos], axis=0)
+    seq_size = lax.axis_size("seq")
+    every_ctx_req, every_ctx_pos = context_places(
+        ctx_lens[0], jnp.arange(seq_size * ctx_count, dtype=jnp.int32)
+    )
+    every_query_req, every_query_pos = query_places(
+        span_lens[0], ctx_lens[0], jnp.arange(seq_size * tok_count, dtype=jnp.int32)
+    )
+    piece_req = jnp.concatenate(
+        [every_ctx_req.reshape(seq_size, ctx_count), every_query_req.reshape(seq_size, tok_count)],
+        axis=1,
+    ).reshape(-1)
+    piece_pos = jnp.concatenate(
+        [every_ctx_pos.reshape(seq_size, ctx_count), every_query_pos.reshape(seq_size, tok_count)],
+        axis=1,
+    ).reshape(-1)
     scale = 1.0 / math.sqrt(head_dim)
     start_state = (
         jnp.full((kv_local, group, tok_count), -1e30, jnp.float32),
@@ -113,10 +126,17 @@
         jnp.zeros((kv_local, group, tok_count, head_dim), jnp.float32),
     )
     state = start_state
-    piece_keys = lax.all_gather(all_keys, "seq", axis=0, tiled=True)
-    piece_values = lax.all_gather(all_values, "seq", axis=0, tiled=True)
-    piece_req = lax.all_gather(key_req, "seq", axis=0, tiled=True)
-    piece_pos = lax.all_gather(key_pos, "seq", axis=0, tiled=True)
+    kv_width = kv_local * head_dim
+    local_kv = jnp.concatenate([all_keys, all_values], axis=1)
+    every_kv = lax.all_to_all(
+        jnp.broadcast_to(local_kv[None], (seq_size,) + local_kv.shape),
+        "seq",
+        split_axis=0,
+        concat_axis=0,
+        tiled=True,
+    )
+    piece_keys = every_kv[:, :, :kv_width].reshape(-1, kv_width)
+    piece_values = every_kv[:, :, kv_width:].reshape(-1, kv_width)
     length = piece_keys.shape[0]
     block = length
     for candidate in (2048, 1280, 1024, 640, 512):
@@ -218,7 +238,6 @@
     layers = earlier_kv.shape[0]
     per_device = tok_count // PAGE
     page_count = layers * per_device
-    seq_size = lax.axis_size("seq")
     page_cap = max(1, page_count // seq_size)
     pages = earlier_kv[:, 0].reshape(layers, per_device, PAGE, kv_local, 2 * head_dim)
     pages = pages.transpose(3, 0, 1, 2, 4).reshape(kv_local, page_count, PAGE, 2 * head_dim)

time: 1130 us -> 629 us (0.56)
  waiting for transfers between devices: 767 us -> 262 us
    all_gather x2 -> x0, waiting for transfers between devices: 297 us -> none  [the longest x1 155 us: shards(): piece_values = lax.all_gather(all_values, 'seq', axis=0, tiled=True)]
    unnamed x5 -> x1, waiting for transfers between devices: 237 us -> 0.02 us
    all_to_all x0 -> x1, waiting for transfers between devices: none -> 50.1 us  [shards(): lax.all_to_all(jnp.broadcast_to(local_kv[None], (seq_size,) + local_kv.sh...]
    reduce_scatter x1, waiting for transfers between devices: 23.6 us -> 2.98 us  [shards(): lax.psum_scatter(jnp.dot(attn, w_out, preferred_element_type=jnp.float32)...]
  transfers between devices with their start and end apart: 8 -> 6, of which waited for: 6 -> 4; matrix products, arithmetic and copies ran while one was open for 9% -> 15% of each run, Pallas kernels for 0% -> 0%
where the time goes in v1:
time: 629 us; the launch traced here: 620 us
  waiting for transfers between devices  262 us (42%)
  matrix products  135 us (21%)
  local copies, waits for them, and re-layouts  93.7 us (15%)
  other arithmetic  65.5 us (10%)
  starting transfers between devices  48 us (8%)
  between operations  14.8 us (2%)
    all_to_all x1, waiting for transfers between devices, shards(): lax.all_to_all(outgoing, ('seq', 'tp', 'pd'), split_axis=0, concat_axis=0...  105 us
    all_to_all x1, waiting for transfers between devices, shards(): lax.all_to_all(expert_mlp(lax.all_to_all(outgoing, ('seq', 'tp', 'pd'), s...  105 us
    all_to_all x1, waiting for transfers between devices, shards(): lax.all_to_all(jnp.broadcast_to(local_kv[None], (seq_size,) + local_kv.sh...  50.1 us
    dot_general x5, matrix products, advance(): jnp.einsum('hgtd,khd->hgtk', queries, key_heads, preferred_element_type=j...  47.9 us
    reduce_sum x5, other arithmetic, advance(): total = factor * total + jnp.sum(expo, axis=-1)  46 us
    dot_general x5, matrix products, advance(): jnp.einsum('hgtk,khd->hgtd', expo.astype(jnp.bfloat16), value_heads, pref...  45.8 us
    scatter x1, local copies, waits for them, and re-layouts, shards(): jnp.zeros((experts * capacity, width), jnp.bfloat16).at[target]  23.8 us
    dot_general x1, matrix products, expert_mlp(): jnp.einsum('sejd,edf->sejf', arrived, w_gate_up, preferred_element_type=j...  16.8 us
  transfers between devices with their start and end apart: 6, of which 4 were waited for; matrix products, arithmetic and copies ran while one was open for 15% of the time, Pallas kernels for 0%

profile of v1, /device:TPU:25, one launch (start us, length us, event | category | flops | bytes accessed | tf_op | source)
XLA Modules:
  0.0 619.9 jit_solution(8546161250482822167)
XLA Ops:
  8.9 1.5 fusion.44
  10.4 2.0 multiply_reduce_fusion.1
  12.4 1.9 convolution_convert_fusion.1
  15.5 2.9 broadcast_in_dim.162
  18.4 8.9 %all-to-all-start = ((bf16[32,320,256]{2,1,0:T(8,128)(2,1)}), bf16[32,320,256]{2,1,0:T(8,128)(2,1)}, u32[]{:S(2)}, u32[]{:S(2)}) async-start(bf16[32,320,256]{2,1,0:T(8,128)(2,1)} %broadcast_in_dim.162), calls=%async_computation | async-start | bytes 10485760 | tf_op jit(solution)/shard_map/all_to_all | solution.py:131
  27.4 6.5 %copy.113 = bf16[1024,2048]{1,0:T(8,128)(2,1)} copy(bf16[1024,2048]{0,1:T(8,128)(2,1)} %bitcast.228) | data formatting | bytes 8388608 | tf_op jit(solution)/shard_map/dot_general | solution.py:90
  33.9 3.9 multiply_reduce_fusion
  39.4 2.1 copy.95
  42.7 50.1 %all-to-all-done = bf16[32,320,256]{2,1,0:T(8,128)(2,1)} async-done(((bf16[32,320,256]{2,1,0:T(8,128)(2,1)}), bf16[32,320,256]{2,1,0:T(8,128)(2,1)}, u32[]{:S(2)}, u32[]{:S(2)}) %all-to-all-start) | async-done | bytes 5242912 | tf_op jit(solution)/shard_map/all_to_all | solution.py:131
  92.9 5.2 fusion.103
  98.1 147.7 %while.15 = (s32[]{:T(128)}, f32[1,8,256]{2,1,0:T(8,128)S(1)}, f32[1,8,256]{2,1,0:T(8,128)S(1)}, f32[1,8,256,128]{3,2,1,0:T(8,128)}, s32[256]{0:T(256)S(1)}, /*i...) while((s32[]{:T(128)}, f32[1,8,256]{2,1,0:T(8,128)S(1)}, ...), condition=%wide.region_16.17_spmd.clone, body=%wide.region_13.16_spmd.clone.sunk | while | flops 2195992576 | bytes 58379428 | solution.py:179
  98.3 1.4 compare_and_fusion.2
  99.7 9.6 %fusion.118 = (f32[8,256]{1,0:T(8,128)S(1)}, f32[2048,8,256]{2,0,1:T(8,128)}) fusion(pred[256,2048]{0,1:T(8,128)(4,1)S(1)} %compare_and_fusion.2, bf16[1,8,256,128]{3,2,1,0:T(8,128)(2,1)} %get-tuple-element.325, bf16[5,2048,128]{2,1,0:T(8,128)(2,1)} %get-tuple-element.324, s32[]{:T(128)} %get-tuple-element.303), kind=kOutput, calls=%fused_computation.9.clone.1 | convolution fusion | flops 1086322688 | bytes 18358784 | tf_op jit(solution)/shard_map/while/body/eval_jaxpr/hgtd,khd->hgtk/dot_general | solution.py:156
  109.3 9.0 %fusion.121 = f32[1,8,256,128]{3,2,1,0:T(8,128)} fusion(f32[2048,8,256]{2,0,1:T(8,128)} %get-tuple-element.288, f32[8,256]{1,0:T(8,128)S(1)} %bitcast.230, pred[256,2048]{0,1:T(8,128)(4,1)} %copy-done.1, f32[1,8,256,128]{3,2,1,0:T(8,128)} %get-tuple-element.306, bf16[5,2048,128]{2,1,0:T(8,128)(2,1)} %get-tuple-element.326, s32[]{:T(128)} %get-tuple-element.303, ...), kind=kOutput, calls=%fused_computation.14.clone.1 | convolution fusion | flops 1091305472 | bytes 19939840 | tf_op jit(solution)/shard_map/while/body/eval_jaxpr/hgtk,khd->hgtd/dot_general | solution.py:164
  118.3 9.2 %fusion.120 = f32[8,256]{1,0:T(8,128)S(1)} fusion(f32[2048,8,256]{2,0,1:T(8,128)} %get-tuple-element.288, f32[8,256]{1,0:T(8,128)S(1)} %bitcast.231, pred[256,2048]{0,1:T(8,128)(4,1)} %copy-done.1), kind=kLoop, calls=%fused_computation.8.clone.1 | loop fusion | flops 16775168 | bytes 17317888 | tf_op jit(solution)/shard_map/while/body/eval_jaxpr/reduce_sum | solution.py:163
  129.0 9.6 %fusion.118 = (f32[8,256]{1,0:T(8,128)S(1)}, f32[2048,8,256]{2,0,1:T(8,128)}) fusion(pred[256,2048]{0,1:T(8,128)(4,1)S(1)} %compare_and_fusion.2, bf16[1,8,256,128]{3,2,1,0:T(8,128)(2,1)} %get-tuple-element.325, bf16[5,2048,128]{2,1,0:T(8,128)(2,1)} %get-tuple-element.324, s32[]{:T(128)} %get-tuple-element.303), kind=kOutput, calls=%fused_computation.9.clone.1 | convolution fusion | flops 1086322688 | bytes 18358784 | tf_op jit(solution)/shard_map/while/body/eval_jaxpr/hgtd,khd->hgtk/dot_general | solution.py:156
  138.6 9.2 %fusion.121 = f32[1,8,256,128]{3,2,1,0:T(8,128)} fusion(f32[2048,8,256]{2,0,1:T(8,128)} %get-tuple-element.288, f32[8,256]{1,0:T(8,128)S(1)} %bitcast.230, pred[256,2048]{0,1:T(8,128)(4,1)} %copy-done.1, f32[1,8,256,128]{3,2,1,0:T(8,128)} %get-tuple-element.306, bf16[5,2048,128]{2,1,0:T(8,128)(2,1)} %get-tuple-element.326, s32[]{:T(128)} %get-tuple-element.303, ...), kind=kOutput, calls=%fused_computation.14.clone.1 | convolution fusion | flops 1091305472 | bytes 19939840 | tf_op jit(solution)/shard_map/while/body/eval_jaxpr/hgtk,khd->hgtd/dot_general | solution.py:164
  147.8 9.2 %fusion.120 = f32[8,256]{1,0:T(8,128)S(1)} fusion(f32[2048,8,256]{2,0,1:T(8,128)} %get-tuple-element.288, f32[8,256]{1,0:T(8,128)S(1)} %bitcast.231, pred[256,2048]{0,1:T(8,128)(4,1)} %copy-done.1), kind=kLoop, calls=%fused_computation.8.clone.1 | loop fusion | flops 16775168 | bytes 17317888 | tf_op jit(solution)/shard_map/while/body/eval_jaxpr/reduce_sum | solution.py:163
  158.6 9.6 %fusion.118 = (f32[8,256]{1,0:T(8,128)S(1)}, f32[2048,8,256]{2,0,1:T(8,128)}) fusion(pred[256,2048]{0,1:T(8,128)(4,1)S(1)} %compare_and_fusion.2, bf16[1,8,256,128]{3,2,1,0:T(8,128)(2,1)} %get-tuple-element.325, bf16[5,2048,128]{2,1,0:T(8,128)(2,1)} %get-tuple-element.324, s32[]{:T(128)} %get-tuple-element.303), kind=kOutput, calls=%fused_computation.9.clone.1 | convolution fusion | flops 1086322688 | bytes 18358784 | tf_op jit(solution)/shard_map/while/body/eval_jaxpr/hgtd,khd->hgtk/dot_general | solution.py:156
  168.2 9.2 %fusion.121 = f32[1,8,256,128]{3,2,1,0:T(8,128)} fusion(f32[2048,8,256]{2,0,1:T(8,128)} %get-tuple-element.288, f32[8,256]{1,0:T(8,128)S(1)} %bitcast.230, pred[256,2048]{0,1:T(8,128)(4,1)} %copy-done.1, f32[1,8,256,128]{3,2,1,0:T(8,128)} %get-tuple-element.306, bf16[5,2048,128]{2,1,0:T(8,128)(2,1)} %get-tuple-element.326, s32[]{:T(128)} %get-tuple-element.303, ...), kind=kOutput, calls=%fused_computation.14.clone.1 | convolution fusion | flops 1091305472 | bytes 19939840 | tf_op jit(solution)/shard_map/while/body/eval_jaxpr/hgtk,khd->hgtd/dot_general | solution.py:164
  177.4 9.2 %fusion.120 = f32[8,256]{1,0:T(8,128)S(1)} fusion(f32[2048,8,256]{2,0,1:T(8,128)} %get-tuple-element.288, f32[8,256]{1,0:T(8,128)S(1)} %bitcast.231, pred[256,2048]{0,1:T(8,128)(4,1)} %copy-done.1), kind=kLoop, calls=%fused_computation.8.clone.1 | loop fusion | flops 16775168 | bytes 17317888 | tf_op jit(solution)/shard_map/while/body/eval_jaxpr/reduce_sum | solution.py:163
  188.1 9.6 %fusion.118 = (f32[8,256]{1,0:T(8,128)S(1)}, f32[2048,8,256]{2,0,1:T(8,128)}) fusion(pred[256,2048]{0,1:T(8,128)(4,1)S(1)} %compare_and_fusion.2, bf16[1,8,256,128]{3,2,1,0:T(8,128)(2,1)} %get-tuple-element.325, bf16[5,2048,128]{2,1,0:T(8,128)(2,1)} %get-tuple-element.324, s32[]{:T(128)} %get-tuple-element.303), kind=kOutput, calls=%fused_computation.9.clone.1 | convolution fusion | flops 1086322688 | bytes 18358784 | tf_op jit(solution)/shard_map/while/body/eval_jaxpr/hgtd,khd->hgtk/dot_general | solution.py:156
  197.7 9.2 %fusion.121 = f32[1,8,256,128]{3,2,1,0:T(8,128)} fusion(f32[2048,8,256]{2,0,1:T(8,128)} %get-tuple-element.288, f32[8,256]{1,0:T(8,128)S(1)} %bitcast.230, pred[256,2048]{0,1:T(8,128)(4,1)} %copy-done.1, f32[1,8,256,128]{3,2,1,0:T(8,128)} %get-tuple-element.306, bf16[5,2048,128]{2,1,0:T(8,128)(2,1)} %get-tuple-element.326, s32[]{:T(128)} %get-tuple-element.303, ...), kind=kOutput, calls=%fused_computation.14.clone.1 | convolution fusion | flops 1091305472 | bytes 19939840 | tf_op jit(solution)/shard_map/while/body/eval_jaxpr/hgtk,khd->hgtd/dot_general | solution.py:164
  206.9 9.2 %fusion.120 = f32[8,256]{1,0:T(8,128)S(1)} fusion(f32[2048,8,256]{2,0,1:T(8,128)} %get-tuple-element.288, f32[8,256]{1,0:T(8,128)S(1)} %bitcast.231, pred[256,2048]{0,1:T(8,128)(4,1)} %copy-done.1), kind=kLoop, calls=%fused_computation.8.clone.1 | loop fusion | flops 16775168 | bytes 17317888 | tf_op jit(solution)/shard_map/while/body/eval_jaxpr/reduce_sum | solution.py:163
  217.7 9.6 %fusion.118 = (f32[8,256]{1,0:T(8,128)S(1)}, f32[2048,8,256]{2,0,1:T(8,128)}) fusion(pred[256,2048]{0,1:T(8,128)(4,1)S(1)} %compare_and_fusion.2, bf16[1,8,256,128]{3,2,1,0:T(8,128)(2,1)} %get-tuple-element.325, bf16[5,2048,128]{2,1,0:T(8,128)(2,1)} %get-tuple-element.324, s32[]{:T(128)} %get-tuple-element.303), kind=kOutput, calls=%fused_computation.9.clone.1 | convolution fusion | flops 1086322688 | bytes 18358784 | tf_op jit(solution)/shard_map/while/body/eval_jaxpr/hgtd,khd->hgtk/dot_general | solution.py:156
  227.3 9.2 %fusion.121 = f32[1,8,256,128]{3,2,1,0:T(8,128)} fusion(f32[2048,8,256]{2,0,1:T(8,128)} %get-tuple-element.288, f32[8,256]{1,0:T(8,128)S(1)} %bitcast.230, pred[256,2048]{0,1:T(8,128)(4,1)} %copy-done.1, f32[1,8,256,128]{3,2,1,0:T(8,128)} %get-tuple-element.306, bf16[5,2048,128]{2,1,0:T(8,128)(2,1)} %get-tuple-element.326, s32[]{:T(128)} %get-tuple-element.303, ...), kind=kOutput, calls=%fused_computation.14.clone.1 | convolution fusion | flops 1091305472 | bytes 19939840 | tf_op jit(solution)/shard_map/while/body/eval_jaxpr/hgtk,khd->hgtd/dot_general | solution.py:164
  236.5 9.2 %fusion.120 = f32[8,256]{1,0:T(8,128)S(1)} fusion(f32[2048,8,256]{2,0,1:T(8,128)} %get-tuple-element.288, f32[8,256]{1,0:T(8,128)S(1)} %bitcast.231, pred[256,2048]{0,1:T(8,128)(4,1)} %copy-done.1), kind=kLoop, calls=%fused_computation.8.clone.1 | loop fusion | flops 16775168 | bytes 17317888 | tf_op jit(solution)/shard_map/while/body/eval_jaxpr/reduce_sum | solution.py:163
  245.7 2.6 copy.96
  249.6 4.4 convolution_convert_fusion
  256.0 9.7 %all-to-all-start.3 = ((s32[1,32,1]{2,0,1:T(1,128)}), s32[1,32,1]{2,0,1:T(1,128)S(1)}, u32[]{:S(2)}, u32[]{:S(2)}) async-start(s32[1,32,1]{2,0,1:T(1,128)} %copy.105), calls=%async_computation.4 | async-start | bytes 32768 | tf_op jit(solution)/shard_map/all_to_all | solution.py:266
  266.8 3.0 reduce-scatter.2.cloned.1.call-done
  269.8 1.5 fusion.60
  273.1 23.8 %scatter_custom_fusion = bf16[1536,2048]{1,0:T(8,128)(2,1)} fusion(s32[1024]{0:T(1024)S(1)} %bitcast.240, bf16[128,2048]{1,0:T(8,128)(2,1)} %fusion.62, s32[1024]{0:T(1024)S(1)} %broadcast_clamp_fusion.1, bf16[]{:T(256)} %constant.112.clone.1), kind=kCustom, calls=%fused_computation.43 | custom fusion | bytes 6291968 | tf_op jit(solution)/shard_map/scatter | solution.py:215
  296.8 10.6 %reshape.819 = bf16[128,1,12,2048]{3,2,0,1:T(8,128)(2,1)} reshape(bf16[1536,2048]{1,0:T(8,128)(2,1)} %scatter_custom_fusion) | data formatting | bytes 12582912 | tf_op jit(solution)/shard_map/reshape | solution.py:216
  307.4 9.8 %all-to-all-start.1 = ((bf16[128,1,12,2048]{3,2,1,0:T(8,128)(2,1)}), bf16[128,1,12,2048]{3,2,1,0:T(8,128)(2,1)}, u32[]{:S(2)}, u32[]{:S(2)}) async-start(bf16[128,1,12,2048]{3,2,1,0:T(8,128)(2,1)} %bitcast.225), calls=%async_computation.2 | async-start | bytes 16777216 | tf_op jit(solution)/shard_map/all_to_all | solution.py:219
  317.2 1.5 broadcast.553
  318.7 3.4 scatter_fusion
  322.2 104.7 %all-to-all-done.1 = bf16[128,1,12,2048]{3,2,1,0:T(8,128)(2,1)} async-done(((bf16[128,1,12,2048]{3,2,1,0:T(8,128)(2,1)}), bf16[128,1,12,2048]{3,2,1,0:T(8,128)(2,1)}, u32[]{:S(2)}, u32[]{:S(2)}) %all-to-all-start.1) | async-done | bytes 6291488 | tf_op jit(solution)/shard_map/all_to_all | solution.py:219
  426.9 9.0 %all-to-all-start.4 = ((bf16[1,32,128,256]{3,2,0,1:T(8,128)(2,1)}), bf16[1,32,128,256]{3,2,0,1:T(8,128)(2,1)}, u32[]{:S(2)}, u32[]{:S(2)}) async-start(bf16[1,32,128,256]{3,2,0,1:T(8,128)(2,1)} %bitcast.226), calls=%async_computation.5 | async-start | bytes 4194304 | tf_op jit(solution)/shard_map/all_to_all | solution.py:265
  435.9 16.8 %fusion.27 = f32[128,1,12,1536]{3,0,2,1:T(8,128)S(1)} fusion(bf16[1,2048,1536]{2,1,0:T(8,128)(2,1)} %param.36, bf16[128,1,12,2048]{3,2,1,0:T(8,128)(2,1)} %all-to-all-done.1), kind=kOutput, calls=%fused_computation.38 | convolution fusion | flops 9663676416 | bytes 22020096 | tf_op jit(solution)/shard_map/sejd,edf->sejf/dot_general | solution.py:50
  452.7 5.4 convert_bitcast_fusion
  458.0 6.8 %copy.101 = bf16[128,1,12,2048]{3,2,1,0:T(8,128)(2,1)} copy(bf16[128,1,12,2048]{3,0,2,1:T(8,128)(2,1)S(1)} %convert_bitcast_fusion) | data formatting | bytes 12582912 | tf_op jit(solution)/shard_map/convert_element_type | solution.py:53
  464.9 10.6 %all-to-all-start.2 = ((bf16[128,1,12,2048]{3,2,1,0:T(8,128)(2,1)}), bf16[128,1,12,2048]{3,2,1,0:T(8,128)(2,1)}, u32[]{:S(2)}, u32[]{:S(2)}) async-start(bf16[128,1,12,2048]{3,2,1,0:T(8,128)(2,1)} %copy.101), calls=%async_computation.3 | async-start | bytes 16777216 | tf_op jit(solution)/shard_map/all_to_all | solution.py:217
  476.3 2.8 fusion.55
  480.5 104.6 %all-to-all-done.2 = bf16[128,1,12,2048]{3,2,1,0:T(8,128)(2,1)} async-done(((bf16[128,1,12,2048]{3,2,1,0:T(8,128)(2,1)}), bf16[128,1,12,2048]{3,2,1,0:T(8,128)(2,1)}, u32[]{:S(2)}, u32[]{:S(2)}) %all-to-all-start.2) | async-done | bytes 6291488 | tf_op jit(solution)/shard_map/all_to_all | solution.py:217
  585.1 10.7 %reshape.824 = bf16[1536,2048]{1,0:T(8,128)(2,1)} reshape(bf16[128,1,12,2048]{3,2,1,0:T(8,128)(2,1)} %all-to-all-done.2) | data formatting | bytes 12582912 | tf_op jit(solution)/shard_map/reshape | solution.py:228
  595.8 12.4 %gather_fusion = bf16[1024,2048]{1,0:T(8,128)(2,1)} fusion(bf16[1536,2048]{1,0:T(8,128)(2,1)} %reshape.824, s32[1024]{0:T(1024)S(1)} %broadcast_clamp_fusion), kind=kCustom, calls=%fused_computation.1 | custom fusion | bytes 8392704 | tf_op jit(solution)/shard_map/gather | solution.py:228
  608.2 3.5 fusion.33
  (136 shorter events, 20.9 us)
Async XLA Ops:
  7.2 445.5 %copy-start = (bf16[1,768,2048]{2,1,0:T(8,128)(2,1)S(1)}, bf16[1,768,2048]{2,1,0:T(8,128)(2,1)}, u32[]{:S(2)}) copy-start(bf16[1,768,2048]{2,1,0:T(8,128)(2,1)} %param.37) | copy-start | bytes 9437188
  7.2 7.2 %copy-start.4 = (bf16[1,64,128]{2,1,0:T(8,128)(2,1)S(1)}, bf16[1,64,128]{2,1,0:T(8,128)(2,1)}, u32[]{:S(2)}) copy-start(bf16[1,64,128]{2,1,0:T(8,128)(2,1)} %param.30) | copy-start | bytes 49156
  7.2 7.3 %copy-start.5 = (bf16[1,64,128]{2,1,0:T(8,128)(2,1)S(1)}, bf16[1,64,128]{2,1,0:T(8,128)(2,1)}, u32[]{:S(2)}) copy-start(bf16[1,64,128]{2,1,0:T(8,128)(2,1)} %param.31) | copy-start | bytes 49156
  7.2 7.5 %copy-start.9 = (s32[1,8]{1,0:T(1,128)S(1)}, s32[1,8]{1,0:T(1,128)}, u32[]{:S(2)}) copy-start(s32[1,8]{1,0:T(1,128)} %param.33) | copy-start | bytes 100
  7.2 7.6 %copy-start.11 = (f32[128]{0:T(128)S(1)}, f32[128]{0:T(128)}, u32[]{:S(2)}) copy-start(f32[128]{0:T(128)} %param.27) | copy-start | bytes 1540
  18.4 74.5 %all-to-all-start = ((bf16[32,320,256]{2,1,0:T(8,128)(2,1)}), bf16[32,320,256]{2,1,0:T(8,128)(2,1)}, u32[]{:S(2)}, u32[]{:S(2)}) async-start(bf16[32,320,256]{2,1,0:T(8,128)(2,1)} %broadcast_in_dim.162), calls=%async_computation | async-start | bytes 10485760 | tf_op jit(solution)/shard_map/all_to_all | solution.py:131
  27.3 242.5 %reduce-scatter.2.cloned.1.call-start = ((), (), s32[]{:S(2)}) async-start(), calls=%async_computation.6 | async-start | bytes 1572864 | tf_op jit(solution)/shard_map/reduce_scatter | solution.py:188
  27.4 6.5 %copy-start.13 = (f32[2048]{0:T(1024)S(1)}, f32[2048]{0:T(1024)}, u32[]{:S(2)}) copy-start(f32[2048]{0:T(1024)} %param.22) | copy-start | bytes 24580
  33.9 4.2 copy-start.12
  99.7 9.6 %copy-start.1 = (pred[256,2048]{0,1:T(8,128)(4,1)}, pred[256,2048]{0,1:T(8,128)(4,1)S(1)}, u32[]{:S(2)}) copy-start(pred[256,2048]{0,1:T(8,128)(4,1)S(1)} %compare_and_fusion.2) | copy-start | bytes 1572868 | tf_op jit(solution)/shard_map/while
  129.0 9.6 %copy-start.1 = (pred[256,2048]{0,1:T(8,128)(4,1)}, pred[256,2048]{0,1:T(8,128)(4,1)S(1)}, u32[]{:S(2)}) copy-start(pred[256,2048]{0,1:T(8,128)(4,1)S(1)} %compare_and_fusion.2) | copy-start | bytes 1572868 | tf_op jit(solution)/shard_map/while
  158.6 9.6 %copy-start.1 = (pred[256,2048]{0,1:T(8,128)(4,1)}, pred[256,2048]{0,1:T(8,128)(4,1)S(1)}, u32[]{:S(2)}) copy-start(pred[256,2048]{0,1:T(8,128)(4,1)S(1)} %compare_and_fusion.2) | copy-start | bytes 1572868 | tf_op jit(solution)/shard_map/while
  188.1 9.6 %copy-start.1 = (pred[256,2048]{0,1:T(8,128)(4,1)}, pred[256,2048]{0,1:T(8,128)(4,1)S(1)}, u32[]{:S(2)}) copy-start(pred[256,2048]{0,1:T(8,128)(4,1)S(1)} %compare_and_fusion.2) | copy-start | bytes 1572868 | tf_op jit(solution)/shard_map/while
  217.7 9.6 %copy-start.1 = (pred[256,2048]{0,1:T(8,128)(4,1)}, pred[256,2048]{0,1:T(8,128)(4,1)S(1)}, u32[]{:S(2)}) copy-start(pred[256,2048]{0,1:T(8,128)(4,1)S(1)} %compare_and_fusion.2) | copy-start | bytes 1572868 | tf_op jit(solution)/shard_map/while
  249.6 4.5 copy-start.10
  249.6 16.1 %copy-start.6 = (s32[1,128,8]{1,2,0:T(8,128)S(1)}, s32[1,128,8]{1,2,0:T(8,128)}, u32[]{:S(2)}) copy-start(s32[1,128,8]{1,2,0:T(8,128)} %param.34) | copy-start | bytes 12292
  254.1 18.0 %copy-start.8 = (f32[2048]{0:T(1024)S(1)}, f32[2048]{0:T(1024)}, u32[]{:S(2)}) copy-start(f32[2048]{0:T(1024)} %param.29) | copy-start | bytes 24580
  256.0 51.4 %all-to-all-start.3 = ((s32[1,32,1]{2,0,1:T(1,128)}), s32[1,32,1]{2,0,1:T(1,128)S(1)}, u32[]{:S(2)}, u32[]{:S(2)}) async-start(s32[1,32,1]{2,0,1:T(1,128)} %copy.105), calls=%async_computation.4 | async-start | bytes 32768 | tf_op jit(solution)/shard_map/all_to_all | solution.py:266
  271.3 0.8 copy-start.2
  307.4 119.4 %all-to-all-start.1 = ((bf16[128,1,12,2048]{3,2,1,0:T(8,128)(2,1)}), bf16[128,1,12,2048]{3,2,1,0:T(8,128)(2,1)}, u32[]{:S(2)}, u32[]{:S(2)}) async-start(bf16[128,1,12,2048]{3,2,1,0:T(8,128)(2,1)} %bitcast.225), calls=%async_computation.2 | async-start | bytes 16777216 | tf_op jit(solution)/shard_map/all_to_all | solution.py:219
  426.9 38.0 %all-to-all-start.4 = ((bf16[1,32,128,256]{3,2,0,1:T(8,128)(2,1)}), bf16[1,32,128,256]{3,2,0,1:T(8,128)(2,1)}, u32[]{:S(2)}, u32[]{:S(2)}) async-start(bf16[1,32,128,256]{3,2,0,1:T(8,128)(2,1)} %bitcast.226), calls=%async_computation.5 | async-start | bytes 4194304 | tf_op jit(solution)/shard_map/all_to_all | solution.py:265
  464.9 10.6 %copy-start.7 = (f32[1,128,8]{1,2,0:T(8,128)S(1)}, f32[1,128,8]{1,2,0:T(8,128)}, u32[]{:S(2)}) copy-start(f32[1,128,8]{1,2,0:T(8,128)} %param.35) | copy-start | bytes 12292
  464.9 120.2 %all-to-all-start.2 = ((bf16[128,1,12,2048]{3,2,1,0:T(8,128)(2,1)}), bf16[128,1,12,2048]{3,2,1,0:T(8,128)(2,1)}, u32[]{:S(2)}, u32[]{:S(2)}) async-start(bf16[128,1,12,2048]{3,2,1,0:T(8,128)(2,1)} %copy.101), calls=%async_computation.3 | async-start | bytes 16777216 | tf_op jit(solution)/shard_map/all_to_all | solution.py:217
  608.2 3.5 copy-start.3
Sparse Core Ops, SparseCore 0:
  254.2 15.5 reduce-scatter.1

commit v2 on v1

--- a/solution.py
+++ b/solution.py
@@ -1,8 +1,11 @@
+import functools
 import math
 
 import jax
 import jax.numpy as jnp
 from jax import lax
+from jax.experimental import pallas as pl
+from jax.experimental.pallas import tpu as pltpu
 from jax.sharding import PartitionSpec as P
 
 PAGE = 128
@@ -44,6 +47,75 @@
     member = request[:, None] == jnp.arange(context_lengths.shape[0], dtype=jnp.int32)[None, :]
     first = jnp.sum(jnp.where(member, starts[None, :], 0), axis=1)
     return (request, places - first)
+
+
+KEY_BLOCK = 512
+
+
+def flash_kernel(nkb, scale, live_ref, qreq_ref, qpos_ref, kreq_ref, kpos_ref, q_ref, k_ref, v_ref, o_ref, m_sc, l_sc, acc_sc):
+    kb = pl.program_id(0)
+
+    @pl.when(kb == 0)
+    def _():
+        m_sc[...] = jnp.full(m_sc.shape, -1e30, jnp.float32)
+        l_sc[...] = jnp.zeros(l_sc.shape, jnp.float32)
+        acc_sc[...] = jnp.zeros(acc_sc.shape, jnp.float32)
+
+    @pl.when(live_ref[kb] > 0)
+    def _():
+        scores = lax.dot_general(
+            q_ref[...], k_ref[...], (((1,), (1,)), ((), ())), preferred_element_type=jnp.float32
+        ) * scale
+        visible = (qreq_ref[...] == kreq_ref[...]) & (kpos_ref[...] <= qpos_ref[...])
+        scores = jnp.where(visible, scores, -jnp.inf)
+        m_old = m_sc[...]
+        m_new = jnp.maximum(m_old, jnp.max(scores, axis=1, keepdims=True))
+        expo = jnp.exp(scores - m_new)
+        factor = jnp.exp(m_old - m_new)
+        l_sc[...] = factor * l_sc[...] + jnp.sum(expo, axis=1, keepdims=True)
+        acc_sc[...] = factor * acc_sc[...] + jnp.dot(
+            expo.astype(jnp.bfloat16), v_ref[...], preferred_element_type=jnp.float32
+        )
+        m_sc[...] = m_new
+
+    @pl.when(kb == nkb - 1)
+    def _():
+        o_ref[...] = (acc_sc[...] / l_sc[...]).astype(o_ref.dtype)
+
+
+def flash_attention(live, qreq, qpos, kreq, kpos, q, k, v, scale):
+    rows, head_dim = q.shape
+    length = k.shape[0]
+    nkb = length // KEY_BLOCK
+    grid_spec = pltpu.PrefetchScalarGridSpec(
+        num_scalar_prefetch=1,
+        grid=(nkb,),
+        in_specs=[
+            pl.BlockSpec((rows, 1), lambda kb, live: (0, 0)),
+            pl.BlockSpec((rows, 1), lambda kb, live: (0, 0)),
+            pl.BlockSpec((1, KEY_BLOCK), lambda kb, live: (0, kb)),
+            pl.BlockSpec((1, KEY_BLOCK), lambda kb, live: (0, kb)),
+            pl.BlockSpec((rows, head_dim), lambda kb, live: (0, 0)),
+            pl.BlockSpec((KEY_BLOCK, head_dim), lambda kb, live: (kb, 0)),
+            pl.BlockSpec((KEY_BLOCK, head_dim), lambda kb, live: (kb, 0)),
+        ],
+        out_specs=pl.BlockSpec((rows, head_dim), lambda kb, live: (0, 0)),
+        scratch_shapes=[
+            pltpu.VMEM((rows, 1), jnp.float32),
+            pltpu.VMEM((rows, 1), jnp.float32),
+            pltpu.VMEM((rows, head_dim), jnp.float32),
+        ],
+    )
+    flops = 4 * rows * length * head_dim
+    return pl.pallas_call(
+        functools.partial(flash_kernel, nkb, scale),
+        grid_spec=grid_spec,
+        out_shape=jax.ShapeDtypeStruct((rows, head_dim), jnp.bfloat16),
+        compiler_params=pltpu.CompilerParams(dimension_semantics=("arbitrary",)),
+        cost_estimate=pl.CostEstimate(
+            flops=flops, transcendentals=rows * length, bytes_accessed=2 * length * head_dim * 2 + 2 * rows * head_dim * 2
+        ),
+    )(live, qreq, qpos, kreq, kpos, q, k, v)
 
 
 def expert_mlp(arrived, w_gate_up, w_down):
@@ -111,21 +183,9 @@
     every_query_req, every_query_pos = query_places(
         span_lens[0], ctx_lens[0], jnp.arange(seq_size * tok_count, dtype=jnp.int32)
     )
-    piece_req = jnp.concatenate(
-        [every_ctx_req.reshape(seq_size, ctx_count), every_query_req.reshape(seq_size, tok_count)],
-        axis=1,
-    ).reshape(-1)
-    piece_pos = jnp.concatenate(
-        [every_ctx_pos.reshape(seq_size, ctx_count), every_query_pos.reshape(seq_size, tok_count)],
-        axis=1,
-    ).reshape(-1)
+    key_req = jnp.concatenate([every_ctx_req, every_query_req], axis=0)
+    key_pos = jnp.concatenate([every_ctx_pos, every_query_pos], axis=0)
     scale = 1.0 / math.sqrt(head_dim)
-    start_state = (
-        jnp.full((kv_local, group, tok_count), -1e30, jnp.float32),
-        jnp.zeros((kv_local, group, tok_count), jnp.float32),
-        jnp.zeros((kv_local, group, tok_count, head_dim), jnp.float32),
-    )
-    state = start_state
     kv_width = kv_local * head_dim
     local_kv = jnp.concatenate([all_keys, all_values], axis=1)
     every_kv = lax.all_to_all(
@@ -135,54 +195,35 @@
         concat_axis=0,
         tiled=True,
     )
-    piece_keys = every_kv[:, :, :kv_width].reshape(-1, kv_width)
-    piece_values = every_kv[:, :, kv_width:].reshape(-1, kv_width)
-    length = piece_keys.shape[0]
-    block = length
-    for candidate in (2048, 1280, 1024, 640, 512):
-        block = candidate
-        break
-    count = length // block
-
-    def advance(running, items):
-        block_keys, block_values, block_req, block_pos = items
-        key_heads = block_keys.reshape(block, kv_local, head_dim)
-        value_heads = block_values.reshape(block, kv_local, head_dim)
-        visible = (query_req[:, None] == block_req[None, :]) & (
-            block_pos[None, :] <= query_pos[:, None]
+    ordered_kv = jnp.concatenate(
+        [every_kv[:, :ctx_count].reshape(-1, 2 * kv_width), every_kv[:, ctx_count:].reshape(-1, 2 * kv_width)],
+        axis=0,
+    )
+    length = ordered_kv.shape[0]
+    seen = (query_req[:, None] == key_req[None, :]) & (key_pos[None, :] <= query_pos[:, None])
+    live = jnp.any(jnp.any(seen, axis=0).reshape(length // KEY_BLOCK, KEY_BLOCK), axis=1).astype(jnp.int32)
+    rows = group * tok_count
+    qreq_rows = jnp.broadcast_to(query_req[None, :], (group, tok_count)).reshape(rows, 1)
+    qpos_rows = jnp.broadcast_to(query_pos[None, :], (group, tok_count)).reshape(rows, 1)
+    heads_out = []
+    for h in range(kv_local):
+        heads_out.append(
+            flash_attention(
+                live,
+                qreq_rows,
+                qpos_rows,
+                key_req.reshape(1, length),
+                key_pos.reshape(1, length),
+                queries[h].reshape(rows, head_dim),
+                ordered_kv[:, h * head_dim:(h + 1) * head_dim],
+                ordered_kv[:, kv_width + h * head_dim:kv_width + (h + 1) * head_dim],
+                scale,
+            ).reshape(group, tok_count, head_dim)
         )
-        largest, total, accum = running
-        scores = (
-            jnp.einsum("hgtd,khd->hgtk", queries, key_heads, preferred_element_type=jnp.float32)
-            * scale
-        )
-        scores = jnp.where(visible[None, None], scores, -jnp.inf)
-        new_largest = jnp.maximum(largest, jnp.max(scores, axis=-1))
-        expo = jnp.exp(scores - new_largest[..., None])
-        factor = jnp.exp(largest - new_largest)
-        total = factor * total + jnp.sum(expo, axis=-1)
-        accum = factor[..., None] * accum + jnp.einsum(
-            "hgtk,khd->hgtd",
-            expo.astype(jnp.bfloat16),
-            value_heads,
-            preferred_element_type=jnp.float32,
-        )
-        running = (new_largest, total, accum)
-        return (running, None)
-
-    stacked = (
-        piece_keys.reshape(count, block, -1),
-        piece_values.reshape(count, block, -1),
-        piece_req.reshape(count, block),
-        piece_pos.reshape(count, block),
-    )
-    state, _ = lax.scan(advance, state, stacked)
-    largest, total, accum = state
     attn = (
-        (accum / total[..., None])
+        jnp.stack(heads_out, axis=0)
         .transpose(2, 0, 1, 3)
         .reshape(tok_count, query_heads * head_dim)
-        .astype(jnp.bfloat16)
     )
     half = tok_count // lax.axis_size("tp")
     proj = lax.psum_scatter(

time: 629 us -> 529 us (0.84)
  matrix products: 135 us -> 41.5 us
  other arithmetic: 65.5 us -> 19.7 us
  Pallas kernels: 0 us -> 35.9 us
  starting transfers between devices: 48 us -> 58.2 us
    dot_general x10 -> x0, matrix products: 93.7 us -> none  [the longest x5 47.9 us: advance(): jnp.einsum('hgtd,khd->hgtk', queries, key_heads, preferred_element_type=j...]
    reduce_sum x5 -> x0, other arithmetic: 46 us -> none  [advance(): total = factor * total + jnp.sum(expo, axis=-1)]
    pallas_call x0 -> x1, Pallas kernels: none -> 35.9 us  [flash_attention(): pl.pallas_call(functools.partial(flash_kernel, nkb, scale), grid_spec=gri...]
    all_to_all x1, starting transfers between devices: 9.72 us -> 19.9 us  [shards(): lax.all_to_all(outgoing_slots, 'seq', split_axis=1, concat_axis=1, tiled=...]
    and x5 -> x0, other arithmetic: 7.24 us -> none  [advance(): (query_req[:, None] == block_req[None, :]) & (block_pos[None, :] <= query...]
  transfers between devices with their start and end apart: 6 -> 6, of which waited for: 4 -> 4; matrix products, arithmetic and copies ran while one was open for 15% -> 19% of each run, Pallas kernels for 0% -> 0%
where the time goes in v2:
time: 529 us; the launch traced here: 522 us
  waiting for transfers between devices  258 us (49%)
  local copies, waits for them, and re-layouts  94.4 us (18%)
  starting transfers between devices  58.2 us (11%)
  matrix products  41.5 us (8%)
  Pallas kernels  35.9 us (7%)
  other arithmetic  19.7 us (4%)
  between operations  14.8 us (3%)
    all_to_all x1, waiting for transfers between devices, shards(): lax.all_to_all(outgoing, ('seq', 'tp', 'pd'), split_axis=0, concat_axis=0...  105 us
    all_to_all x1, waiting for transfers between devices, shards(): lax.all_to_all(expert_mlp(lax.all_to_all(outgoing, ('seq', 'tp', 'pd'), s...  105 us
    all_to_all x1, waiting for transfers between devices, shards(): lax.all_to_all(jnp.broadcast_to(local_kv[None], (seq_size,) + local_kv.sh...  44.3 us
    pallas_call x1, Pallas kernels, flash_attention(): pl.pallas_call(functools.partial(flash_kernel, nkb, scale), grid_spec=gri...  35.9 us
    scatter x1, local copies, waits for them, and re-layouts, shards(): jnp.zeros((experts * capacity, width), jnp.bfloat16).at[target]  24 us
    all_to_all x1, starting transfers between devices, shards(): lax.all_to_all(outgoing_slots, 'seq', split_axis=1, concat_axis=1, tiled=...  19.9 us
    dot_general x1, matrix products, expert_mlp(): jnp.einsum('sejd,edf->sejf', arrived, w_gate_up, preferred_element_type=j...  16.8 us
    gather x1, local copies, waits for them, and re-layouts, shards(): gathered = returned.reshape(experts * capacity, width)[target]  12.4 us
  transfers between devices with their start and end apart: 6, of which 4 were waited for; matrix products, arithmetic and copies ran while one was open for 19% of the time, Pallas kernels for 0%

profile of v2, /device:TPU:25, one launch (start us, length us, event | category | flops | bytes accessed | tf_op | source)
XLA Modules:
  0.0 522.4 jit_solution(14940592368725481759)
XLA Ops:
  7.3 1.0 reduce-window.6
  8.2 0.7 fusion.74
  8.9 1.5 fusion.22
  10.4 2.0 multiply_reduce_fusion.1
  12.4 1.9 convolution_convert_fusion.1
  15.5 2.9 broadcast_in_dim.154
  18.4 8.9 %all-to-all-start = ((bf16[32,320,256]{2,1,0:T(8,128)(2,1)}), bf16[32,320,256]{2,1,0:T(8,128)(2,1)}, u32[]{:S(2)}, u32[]{:S(2)}) async-start(bf16[32,320,256]{2,1,0:T(8,128)(2,1)} %broadcast_in_dim.154), calls=%async_computation | async-start | bytes 10485760 | tf_op jit(solution)/shard_map/all_to_all | solution.py:191
  27.4 6.5 %copy.115 = bf16[1024,2048]{1,0:T(8,128)(2,1)} copy(bf16[1024,2048]{0,1:T(8,128)(2,1)} %bitcast.176) | data formatting | bytes 8388608 | tf_op jit(solution)/shard_map/dot_general | solution.py:162
  33.9 3.9 multiply_reduce_fusion
  38.5 0.8 maximum_bitcast_fusion
  39.3 2.0 copy.92
  42.2 3.0 and_reduce_fusion
  45.9 1.4 copy.119
  47.3 1.3 copy.117
  48.6 44.3 %all-to-all-done = bf16[32,320,256]{2,1,0:T(8,128)(2,1)} async-done(((bf16[32,320,256]{2,1,0:T(8,128)(2,1)}), bf16[32,320,256]{2,1,0:T(8,128)(2,1)}, u32[]{:S(2)}, u32[]{:S(2)}) %all-to-all-start) | async-done | bytes 5242912 | tf_op jit(solution)/shard_map/all_to_all | solution.py:191
  92.9 2.5 slice.53
  95.4 1.3 slice.52
  96.7 5.4 %pad_maximum_fusion = (bf16[10240,128]{1,0:T(8,128)(2,1)}, bf16[10240,128]{1,0:T(8,128)(2,1)}) fusion(bf16[8192,256]{1,0:T(8,128)(2,1)S(1)} %bitcast.173, bf16[2048,256]{1,0:T(8,128)(2,1)S(1)} %bitcast.175), kind=kLoop, calls=%fused_computation.29 | loop fusion | flops 10485760 | bytes 10485760 | tf_op jit(solution)/shard_map/concatenate | solution.py:198
  102.1 35.9 %shard_map.194 = bf16[2048,128]{1,0:T(8,128)(2,1)} custom-call(s32[20]{0:T(128)} %convert_element_type.133.live_ref, s32[2048,1]{1,0:T(8,128)} %bitcast.180, s32[2048,1]{1,0:T(8,128)} %bitcast.179, s32[1,10240]{1,0:T(1,128)} %bitcast.184, s32[1,10240]{1,0:T(1,128)} %bitcast.185, bf16[2048,128]{1,0:T(8,128)(2,1)} %bitcast.181, ...), custom_call_target="tpu_custom_call" | custom-call | flops 10737418240 | bytes 6291456 | tf_op jit(solution)/shard_map/pallas_call | solution.py:110
  138.0 2.0 copy.99
  140.0 4.6 convolution_convert_fusion
  145.3 0.6 scatter_custom_fusion.1
  145.9 0.7 copy.108
  146.6 19.9 %all-to-all-start.3 = ((s32[1,32,1]{2,0,1:T(1,128)}), s32[1,32,1]{2,0,1:T(1,128)S(1)}, u32[]{:S(2)}, u32[]{:S(2)}) async-start(s32[1,32,1]{2,0,1:T(1,128)} %copy.108), calls=%async_computation.4 | async-start | bytes 32768 | tf_op jit(solution)/shard_map/all_to_all | solution.py:307
  166.7 0.6 fusion.37
  167.6 4.5 reduce-scatter.2.cloned.1.call-done
  172.1 1.5 fusion.38
  173.6 0.8 copy-done.1
  174.3 1.0 fusion.40
  175.3 24.0 %scatter_custom_fusion = bf16[1536,2048]{1,0:T(8,128)(2,1)} fusion(s32[1024]{0:T(1024)S(1)} %bitcast.190, bf16[128,2048]{1,0:T(8,128)(2,1)} %fusion.40, s32[1024]{0:T(1024)S(1)} %broadcast_clamp_fusion.1, bf16[]{:T(256)} %constant.90.clone.1), kind=kCustom, calls=%fused_computation.18 | custom fusion | bytes 6291968 | tf_op jit(solution)/shard_map/scatter | solution.py:256
  199.3 10.6 %reshape.754 = bf16[128,1,12,2048]{3,2,0,1:T(8,128)(2,1)} reshape(bf16[1536,2048]{1,0:T(8,128)(2,1)} %scatter_custom_fusion) | data formatting | bytes 12582912 | tf_op jit(solution)/shard_map/reshape | solution.py:257
  209.9 9.8 %all-to-all-start.1 = ((bf16[128,1,12,2048]{3,2,1,0:T(8,128)(2,1)}), bf16[128,1,12,2048]{3,2,1,0:T(8,128)(2,1)}, u32[]{:S(2)}, u32[]{:S(2)}) async-start(bf16[128,1,12,2048]{3,2,1,0:T(8,128)(2,1)} %bitcast.172), calls=%async_computation.2 | async-start | bytes 16777216 | tf_op jit(solution)/shard_map/all_to_all | solution.py:260
  219.7 1.6 broadcast.507
  221.3 3.4 scatter_fusion
  224.7 104.6 %all-to-all-done.1 = bf16[128,1,12,2048]{3,2,1,0:T(8,128)(2,1)} async-done(((bf16[128,1,12,2048]{3,2,1,0:T(8,128)(2,1)}), bf16[128,1,12,2048]{3,2,1,0:T(8,128)(2,1)}, u32[]{:S(2)}, u32[]{:S(2)}) %all-to-all-start.1) | async-done | bytes 6291488 | tf_op jit(solution)/shard_map/all_to_all | solution.py:260
  329.3 9.0 %all-to-all-start.4 = ((bf16[1,32,128,256]{3,2,0,1:T(8,128)(2,1)}), bf16[1,32,128,256]{3,2,0,1:T(8,128)(2,1)}, u32[]{:S(2)}, u32[]{:S(2)}) async-start(bf16[1,32,128,256]{3,2,0,1:T(8,128)(2,1)} %bitcast.174), calls=%async_computation.5 | async-start | bytes 4194304 | tf_op jit(solution)/shard_map/all_to_all | solution.py:306
  338.4 16.8 %fusion.4 = f32[128,1,12,1536]{3,0,2,1:T(8,128)S(1)} fusion(bf16[1,2048,1536]{2,1,0:T(8,128)(2,1)} %param.34, bf16[128,1,12,2048]{3,2,1,0:T(8,128)(2,1)} %all-to-all-done.1), kind=kOutput, calls=%fused_computation.11 | convolution fusion | flops 9663676416 | bytes 22020096 | tf_op jit(solution)/shard_map/sejd,edf->sejf/dot_general | solution.py:122
  355.1 5.4 %convert_bitcast_fusion = bf16[128,1,12,2048]{3,0,2,1:T(8,128)(2,1)S(1)} fusion(bf16[1,768,2048]{2,1,0:T(8,128)(2,1)S(1)} %copy-done, f32[128,1,12,1536]{3,0,2,1:T(8,128)S(1)} %fusion.4), kind=kOutput, calls=%fused_computation.10 | convolution fusion | flops 4842061824 | bytes 18874368 | tf_op jit(solution)/shard_map/sejf,efd->sejd/dot_general | solution.py:125
  360.5 6.9 %copy.104 = bf16[128,1,12,2048]{3,2,1,0:T(8,128)(2,1)} copy(bf16[128,1,12,2048]{3,0,2,1:T(8,128)(2,1)S(1)} %convert_bitcast_fusion) | data formatting | bytes 12582912 | tf_op jit(solution)/shard_map/convert_element_type | solution.py:125
  367.4 10.6 %all-to-all-start.2 = ((bf16[128,1,12,2048]{3,2,1,0:T(8,128)(2,1)}), bf16[128,1,12,2048]{3,2,1,0:T(8,128)(2,1)}, u32[]{:S(2)}, u32[]{:S(2)}) async-start(bf16[128,1,12,2048]{3,2,1,0:T(8,128)(2,1)} %copy.104), calls=%async_computation.3 | async-start | bytes 16777216 | tf_op jit(solution)/shard_map/all_to_all | solution.py:258
  378.2 0.7 reduce.4
  378.9 2.8 fusion.33
  381.7 1.3 copy.111
  383.0 104.6 %all-to-all-done.2 = bf16[128,1,12,2048]{3,2,1,0:T(8,128)(2,1)} async-done(((bf16[128,1,12,2048]{3,2,1,0:T(8,128)(2,1)}), bf16[128,1,12,2048]{3,2,1,0:T(8,128)(2,1)}, u32[]{:S(2)}, u32[]{:S(2)}) %all-to-all-start.2) | async-done | bytes 6291488 | tf_op jit(solution)/shard_map/all_to_all | solution.py:258
  487.7 10.7 %reshape.759 = bf16[1536,2048]{1,0:T(8,128)(2,1)} reshape(bf16[128,1,12,2048]{3,2,1,0:T(8,128)(2,1)} %all-to-all-done.2) | data formatting | bytes 12582912 | tf_op jit(solution)/shard_map/reshape | solution.py:269
  498.4 12.4 %gather_fusion = bf16[1024,2048]{1,0:T(8,128)(2,1)} fusion(bf16[1536,2048]{1,0:T(8,128)(2,1)} %reshape.759, s32[1024]{0:T(1024)S(1)} %broadcast_clamp_fusion), kind=kCustom, calls=%fused_computation.1 | custom fusion | bytes 8392704 | tf_op jit(solution)/shard_map/gather | solution.py:269
  510.8 3.5 fusion.10
  514.3 1.1 fusion.48
  (90 shorter events, 4.6 us)
Async XLA Ops:
  7.2 348.0 %copy-start = (bf16[1,768,2048]{2,1,0:T(8,128)(2,1)S(1)}, bf16[1,768,2048]{2,1,0:T(8,128)(2,1)}, u32[]{:S(2)}) copy-start(bf16[1,768,2048]{2,1,0:T(8,128)(2,1)} %param.35) | copy-start | bytes 9437188
  7.2 7.2 %copy-start.5 = (bf16[1,64,128]{2,1,0:T(8,128)(2,1)S(1)}, bf16[1,64,128]{2,1,0:T(8,128)(2,1)}, u32[]{:S(2)}) copy-start(bf16[1,64,128]{2,1,0:T(8,128)(2,1)} %param.28) | copy-start | bytes 49156
  7.2 7.3 %copy-start.6 = (bf16[1,64,128]{2,1,0:T(8,128)(2,1)S(1)}, bf16[1,64,128]{2,1,0:T(8,128)(2,1)}, u32[]{:S(2)}) copy-start(bf16[1,64,128]{2,1,0:T(8,128)(2,1)} %param.29) | copy-start | bytes 49156
  7.2 7.5 %copy-start.10 = (s32[1,8]{1,0:T(1,128)S(1)}, s32[1,8]{1,0:T(1,128)}, u32[]{:S(2)}) copy-start(s32[1,8]{1,0:T(1,128)} %param.31) | copy-start | bytes 100
  7.2 7.6 %copy-start.12 = (f32[128]{0:T(128)S(1)}, f32[128]{0:T(128)}, u32[]{:S(2)}) copy-start(f32[128]{0:T(128)} %param.25) | copy-start | bytes 1540
  18.4 74.5 %all-to-all-start = ((bf16[32,320,256]{2,1,0:T(8,128)(2,1)}), bf16[32,320,256]{2,1,0:T(8,128)(2,1)}, u32[]{:S(2)}, u32[]{:S(2)}) async-start(bf16[32,320,256]{2,1,0:T(8,128)(2,1)} %broadcast_in_dim.154), calls=%async_computation | async-start | bytes 10485760 | tf_op jit(solution)/shard_map/all_to_all | solution.py:191
  27.3 144.8 %reduce-scatter.2.cloned.1.call-start = ((), (), s32[]{:S(2)}) async-start(), calls=%async_computation.6 | async-start | bytes 1572864 | tf_op jit(solution)/shard_map/reduce_scatter | solution.py:229
  27.3 6.5 %copy-start.14 = (f32[2048]{0:T(1024)S(1)}, f32[2048]{0:T(1024)}, u32[]{:S(2)}) copy-start(f32[2048]{0:T(1024)} %param.20) | copy-start | bytes 24580
  33.9 4.2 copy-start.13
  42.2 53.2 %copy-start.3 = (s32[10240]{0:T(1024)}, s32[10240]{0:T(1024)S(1)}, u32[]{:S(2)}) copy-start(s32[10240]{0:T(1024)S(1)} %get-tuple-element.32) | copy-start | bytes 122884
  42.2 53.2 %copy-start.4 = (s32[10240]{0:T(1024)}, s32[10240]{0:T(1024)S(1)}, u32[]{:S(2)}) copy-start(s32[10240]{0:T(1024)S(1)} %get-tuple-element.33) | copy-start | bytes 122884
  140.0 4.6 copy-start.11
  140.0 26.4 %copy-start.7 = (s32[1,128,8]{1,2,0:T(8,128)S(1)}, s32[1,128,8]{1,2,0:T(8,128)}, u32[]{:S(2)}) copy-start(s32[1,128,8]{1,2,0:T(8,128)} %param.32) | copy-start | bytes 12292
  144.6 29.7 %copy-start.9 = (f32[2048]{0:T(1024)S(1)}, f32[2048]{0:T(1024)}, u32[]{:S(2)}) copy-start(f32[2048]{0:T(1024)} %param.27) | copy-start | bytes 24580
  146.6 63.3 %all-to-all-start.3 = ((s32[1,32,1]{2,0,1:T(1,128)}), s32[1,32,1]{2,0,1:T(1,128)S(1)}, u32[]{:S(2)}, u32[]{:S(2)}) async-start(s32[1,32,1]{2,0,1:T(1,128)} %copy.108), calls=%async_computation.4 | async-start | bytes 32768 | tf_op jit(solution)/shard_map/all_to_all | solution.py:307
  173.5 0.8 copy-start.1
  209.9 119.4 %all-to-all-start.1 = ((bf16[128,1,12,2048]{3,2,1,0:T(8,128)(2,1)}), bf16[128,1,12,2048]{3,2,1,0:T(8,128)(2,1)}, u32[]{:S(2)}, u32[]{:S(2)}) async-start(bf16[128,1,12,2048]{3,2,1,0:T(8,128)(2,1)} %bitcast.172), calls=%async_computation.2 | async-start | bytes 16777216 | tf_op jit(solution)/shard_map/all_to_all | solution.py:260
  329.3 38.1 %all-to-all-start.4 = ((bf16[1,32,128,256]{3,2,0,1:T(8,128)(2,1)}), bf16[1,32,128,256]{3,2,0,1:T(8,128)(2,1)}, u32[]{:S(2)}, u32[]{:S(2)}) async-start(bf16[1,32,128,256]{3,2,0,1:T(8,128)(2,1)} %bitcast.174), calls=%async_computation.5 | async-start | bytes 4194304 | tf_op jit(solution)/shard_map/all_to_all | solution.py:306
  367.4 10.6 %copy-start.8 = (f32[1,128,8]{1,2,0:T(8,128)S(1)}, f32[1,128,8]{1,2,0:T(8,128)}, u32[]{:S(2)}) copy-start(f32[1,128,8]{1,2,0:T(8,128)} %param.33) | copy-start | bytes 12292
  367.4 120.2 %all-to-all-start.2 = ((bf16[128,1,12,2048]{3,2,1,0:T(8,128)(2,1)}), bf16[128,1,12,2048]{3,2,1,0:T(8,128)(2,1)}, u32[]{:S(2)}, u32[]{:S(2)}) async-start(bf16[128,1,12,2048]{3,2,1,0:T(8,128)(2,1)} %copy.104), calls=%async_computation.3 | async-start | bytes 16777216 | tf_op jit(solution)/shard_map/all_to_all | solution.py:258
  510.8 3.5 copy-start.2
Sparse Core Ops, SparseCore 0:
  144.8 27.2 reduce-scatter.1

commit v3 on v2

--- a/solution.py
+++ b/solution.py
@@ -253,28 +253,33 @@
     rank = jnp.sum(before * picks.astype(jnp.float32), axis=1).astype(jnp.int32)
     target = row_ids * capacity + rank
     row_token = jnp.arange(row_count, dtype=jnp.int32) // top
-    outgoing = jnp.zeros((experts * capacity, width), jnp.bfloat16).at[target].set(mixed[row_token])
-    outgoing = outgoing.reshape(device_count, exp_local, capacity, width)
+    lanes = 128
+    chunks = width // lanes
+    moe_axes = ("seq", "tp", "pd")
+    outgoing = (
+        jnp.zeros((experts * capacity, chunks, lanes), jnp.bfloat16)
+        .at[target]
+        .set(mixed.reshape(half, chunks, lanes)[row_token])
+    )
+    outgoing = outgoing.reshape(device_count, exp_local * capacity * chunks, lanes)
+    arrived = lax.all_to_all(outgoing, moe_axes, split_axis=0, concat_axis=0, tiled=True)
+    done = expert_mlp(arrived.reshape(device_count, exp_local, capacity, width), w_gate_up, w_down)
     returned = lax.all_to_all(
-        expert_mlp(
-            lax.all_to_all(outgoing, ("seq", "tp", "pd"), split_axis=0, concat_axis=0, tiled=True),
-            w_gate_up,
-            w_down,
-        ),
-        ("seq", "tp", "pd"),
+        done.reshape(device_count, exp_local * capacity * chunks, lanes),
+        moe_axes,
         split_axis=0,
         concat_axis=0,
         tiled=True,
     )
-    gathered = returned.reshape(experts * capacity, width)[target]
+    gathered = returned.reshape(experts * capacity, chunks, lanes)[target]
     weights = route_weights[0]
     weights = weights / jnp.sum(weights, axis=-1, keepdims=True)
     moe = jnp.einsum(
-        "tkd,tk->td",
-        gathered.reshape(half, top, width),
+        "tkcl,tk->tcl",
+        gathered.reshape(half, top, chunks, lanes),
         weights,
         preferred_element_type=jnp.float32,
-    )
+    ).reshape(half, width)
     layer_out = (resid.astype(jnp.float32) + moe).astype(jnp.bfloat16)[None]
     layers = earlier_kv.shape[0]
     per_device = tok_count // PAGE

time: 529 us -> 552 us (1.043)
  local copies, waits for them, and re-layouts: 94.4 us -> 186 us
  waiting for transfers between devices: 258 us -> 220 us
  starting transfers between devices: 58.2 us -> 42.5 us
  Pallas kernels: 35.9 us -> 23.7 us
    scatter x1, local copies, waits for them, and re-layouts: 24 us -> 104 us  [shards(): outgoing = jnp.zeros((experts * capacity, chunks, lanes), jnp.bfloat16).a...]
    all_to_all x2, waiting for transfers between devices: 209 us -> 150 us  [the longest x1 76.8 us: shards(): lax.all_to_all(outgoing, moe_axes, split_axis=0, concat_axis=0, tiled=True)]
    reduce_scatter x1, waiting for transfers between devices: 4.49 us -> 25 us  [shards(): lax.psum_scatter(jnp.dot(attn, w_out, preferred_element_type=jnp.float32)...]
    all_to_all x1, starting transfers between devices: 19.9 us -> 4.36 us  [shards(): lax.all_to_all(outgoing_slots, 'seq', split_axis=1, concat_axis=1, tiled=...]
    reshape x2 -> x1, local copies, waits for them, and re-layouts: 21.3 us -> 8.99 us  [shards(): done.reshape(device_count, exp_local * capacity * chunks, lanes)]
    pallas_call x1, Pallas kernels: 35.9 us -> 23.7 us  [flash_attention(): pl.pallas_call(functools.partial(flash_kernel, nkb, scale), grid_spec=gri...]
    all_to_all x0 -> x1, local copies, waits for them, and re-layouts: none -> 9.17 us  [shards(): lax.all_to_all(outgoing, moe_axes, split_axis=0, concat_axis=0, tiled=True)]
    gather x1 -> x2, local copies, waits for them, and re-layouts: 12.4 us -> 20.6 us  [the longest x1 11.2 us: shards(): gathered = returned.reshape(experts * capacity, chunks, lanes)[target]]
  transfers between devices with their start and end apart: 6 -> 6, of which waited for: 4 -> 4; matrix products, arithmetic and copies ran while one was open for 19% -> 15% of each run, Pallas kernels for 0% -> 0%
where the time goes in v3:
time: 552 us; the launch traced here: 546 us
  waiting for transfers between devices  220 us (40%)
  local copies, waits for them, and re-layouts  186 us (34%)
  starting transfers between devices  42.5 us (8%)
  matrix products  40.9 us (7%)
  Pallas kernels  23.7 us (4%)
  other arithmetic  18.9 us (3%)
  between operations  14.6 us (3%)
    scatter x1, local copies, waits for them, and re-layouts, shards(): outgoing = jnp.zeros((experts * capacity, chunks, lanes), jnp.bfloat16).a...  104 us
    all_to_all x1, waiting for transfers between devices, shards(): lax.all_to_all(outgoing, moe_axes, split_axis=0, concat_axis=0, tiled=True)  76.8 us
    all_to_all x1, waiting for transfers between devices, shards(): lax.all_to_all(done.reshape(device_count, exp_local * capacity * chunks,...  73.7 us
    all_to_all x1, waiting for transfers between devices, shards(): lax.all_to_all(jnp.broadcast_to(local_kv[None], (seq_size,) + local_kv.sh...  44.2 us
    reduce_scatter x1, waiting for transfers between devices, shards(): lax.psum_scatter(jnp.dot(attn, w_out, preferred_element_type=jnp.float32)...  25 us
    pallas_call x1, Pallas kernels, flash_attention(): pl.pallas_call(functools.partial(flash_kernel, nkb, scale), grid_spec=gri...  23.7 us
    dot_general x1, matrix products, expert_mlp(): jnp.einsum('sejd,edf->sejf', arrived, w_gate_up, preferred_element_type=j...  14.5 us
    all_to_all x1, starting transfers between devices, shards(): lax.all_to_all(done.reshape(device_count, exp_local * capacity * chunks,...  11.8 us
  transfers between devices with their start and end apart: 6, of which 4 were waited for; matrix products, arithmetic and copies ran while one was open for 15% of the time, Pallas kernels for 0%

profile of v3, /device:TPU:25, one launch (start us, length us, event | category | flops | bytes accessed | tf_op | source)
XLA Modules:
  0.0 546.0 jit_solution(142564242248771082)
XLA Ops:
  7.3 1.0 reduce-window.6
  8.2 0.7 fusion.68
  8.9 1.5 fusion.15
  10.4 2.0 multiply_reduce_fusion.1
  12.4 1.9 convolution_convert_fusion.1
  15.5 2.9 broadcast_in_dim.154
  18.4 8.9 %all-to-all-start = ((bf16[32,320,256]{2,1,0:T(8,128)(2,1)}), bf16[32,320,256]{2,1,0:T(8,128)(2,1)}, u32[]{:S(2)}, u32[]{:S(2)}) async-start(bf16[32,320,256]{2,1,0:T(8,128)(2,1)} %broadcast_in_dim.154), calls=%async_computation | async-start | bytes 10485760 | tf_op jit(solution)/shard_map/all_to_all | solution.py:191
  27.4 6.5 %copy.140 = bf16[1024,2048]{1,0:T(8,128)(2,1)} copy(bf16[1024,2048]{0,1:T(8,128)(2,1)} %bitcast.182) | data formatting | bytes 8388608 | tf_op jit(solution)/shard_map/dot_general | solution.py:162
  33.9 3.9 multiply_reduce_fusion
  38.5 0.8 maximum_bitcast_fusion
  39.3 2.0 copy.114
  42.2 3.0 and_reduce_fusion
  45.9 1.4 copy.144
  47.3 1.3 copy.142
  48.7 44.2 %all-to-all-done = bf16[32,320,256]{2,1,0:T(8,128)(2,1)} async-done(((bf16[32,320,256]{2,1,0:T(8,128)(2,1)}), bf16[32,320,256]{2,1,0:T(8,128)(2,1)}, u32[]{:S(2)}, u32[]{:S(2)}) %all-to-all-start) | async-done | bytes 5242912 | tf_op jit(solution)/shard_map/all_to_all | solution.py:191
  92.9 2.5 slice.53
  95.4 1.3 slice.52
  96.7 5.4 pad_maximum_fusion
  102.1 23.7 %shard_map.194 = bf16[2048,128]{1,0:T(8,128)(2,1)} custom-call(s32[20]{0:T(128)} %convert_element_type.133.live_ref, s32[2048,1]{1,0:T(8,128)} %bitcast.187, s32[2048,1]{1,0:T(8,128)} %bitcast.186, s32[1,10240]{1,0:T(1,128)} %bitcast.192, s32[1,10240]{1,0:T(1,128)} %bitcast.193, bf16[2048,128]{1,0:T(8,128)(2,1)} %bitcast.189, ...), custom_call_target="tpu_custom_call" | custom-call | flops 10737418240 | bytes 6291456 | tf_op jit(solution)/shard_map/pallas_call | solution.py:110
  125.8 2.0 copy.121
  127.8 4.6 convolution_convert_fusion
  133.6 25.0 %reduce-scatter.2.cloned.1.call-done = bf16[128,2048]{1,0:T(8,128)(2,1)} async-done(((bf16[256,2048]{1,0:T(8,128)(2,1)}), bf16[128,2048]{1,0:T(8,128)(2,1)}) %reduce-scatter.2.cloned.1.call-update) | async-done | bytes 524304 | tf_op jit(solution)/shard_map/reduce_scatter | solution.py:229
  158.6 1.5 fusion.31
  160.1 0.8 copy-done.1
  161.1 0.9 copy.145
  162.0 9.4 %gather_fusion = bf16[1024,16,128]{2,1,0:T(8,128)(2,1)} fusion(bf16[128,16,128]{2,1,0:T(8,128)(2,1)} %bitcast.176, s32[1024]{0:T(1024)S(1)} %broadcast_clamp_fusion.1), kind=kCustom, calls=%fused_computation | custom fusion | bytes 8392704 | tf_op jit(solution)/shard_map/gather | solution.py:262
  171.4 3.2 broadcast_in_dim.155
  174.6 104.4 %scatter_fusion = bf16[1536,16,128]{2,1,0:T(8,128)(2,1)} fusion(bf16[1536,16,128]{2,1,0:T(8,128)(2,1)} %broadcast_in_dim.155, s32[1024]{0:T(1024)S(1)} %bitcast.196, bf16[1024,16,128]{2,1,0:T(8,128)(2,1)} %gather_fusion), kind=kCustom, calls=%fused_computation.2 | custom fusion | bytes 12587008 | tf_op jit(solution)/shard_map/scatter | solution.py:262
  278.9 9.7 %all-to-all-start.1 = ((bf16[128,192,128]{2,1,0:T(8,128)(2,1)}), bf16[128,192,128]{2,1,0:T(8,128)(2,1)}, u32[]{:S(2)}, u32[]{:S(2)}) async-start(bf16[128,192,128]{2,1,0:T(8,128)(2,1)} %bitcast.175), calls=%async_computation.2 | async-start | bytes 12582912 | tf_op jit(solution)/shard_map/all_to_all | solution.py:265
  289.8 0.7 copy.131
  290.5 76.8 %all-to-all-done.1 = bf16[128,192,128]{2,1,0:T(8,128)(2,1)} async-done(((bf16[128,192,128]{2,1,0:T(8,128)(2,1)}), bf16[128,192,128]{2,1,0:T(8,128)(2,1)}, u32[]{:S(2)}, u32[]{:S(2)}) %all-to-all-start.1) | async-done | bytes 6291488 | tf_op jit(solution)/shard_map/all_to_all | solution.py:265
  367.3 4.4 all-to-all-start.3
  371.7 1.6 broadcast.507
  373.3 3.4 scatter_fusion.1
  376.7 9.2 %copy.124 = bf16[128,192,128]{0,2,1:T(8,128)(2,1)} copy(bf16[128,192,128]{2,1,0:T(8,128)(2,1)} %all-to-all-done.1) | data formatting | bytes 12582912 | tf_op jit(solution)/shard_map/all_to_all | solution.py:265
  385.9 7.8 %all-to-all-start.4 = ((bf16[1,32,128,256]{3,2,0,1:T(8,128)(2,1)}), bf16[1,32,128,256]{3,2,0,1:T(8,128)(2,1)}, u32[]{:S(2)}, u32[]{:S(2)}) async-start(bf16[1,32,128,256]{3,2,0,1:T(8,128)(2,1)} %bitcast.179), calls=%async_computation.5 | async-start | bytes 4194304 | tf_op jit(solution)/shard_map/all_to_all | solution.py:311
  393.6 14.5 %fusion.2 = f32[128,1,12,1536]{3,0,2,1:T(8,128)S(1)} fusion(bf16[128,12,2048]{0,2,1:T(8,128)(2,1)} %bitcast.180, bf16[1,2048,1536]{2,1,0:T(8,128)(2,1)} %param.34), kind=kOutput, calls=%fused_computation.9 | convolution fusion | flops 9663676416 | bytes 22020096 | tf_op jit(solution)/shard_map/sejd,edf->sejf/dot_general | solution.py:122
  408.2 7.1 %convert_bitcast_fusion = bf16[128,1,12,2048]{3,0,2,1:T(8,128)(2,1)} fusion(bf16[1,768,2048]{2,1,0:T(8,128)(2,1)S(1)} %copy-done, f32[128,1,12,1536]{3,0,2,1:T(8,128)S(1)} %fusion.2), kind=kOutput, calls=%fused_computation.8 | convolution fusion | flops 4842061824 | bytes 18874368 | tf_op jit(solution)/shard_map/sejf,efd->sejd/dot_general | solution.py:125
  415.2 8.6 %copy.126 = bf16[128,1,12,2048]{0,3,2,1:T(8,128)(2,1)} copy(bf16[128,1,12,2048]{3,0,2,1:T(8,128)(2,1)} %convert_bitcast_fusion) | data formatting | bytes 12582912 | tf_op jit(solution)/shard_map/convert_element_type | solution.py:125
  423.9 9.0 %copy.127 = bf16[128,192,128]{2,1,0:T(8,128)(2,1)} copy(bf16[128,192,128]{0,2,1:T(8,128)(2,1)} %bitcast.177) | data formatting | bytes 12582912 | tf_op jit(solution)/shard_map/reshape | solution.py:268
  432.8 11.8 %all-to-all-start.2 = ((bf16[128,192,128]{2,1,0:T(8,128)(2,1)}), bf16[128,192,128]{2,1,0:T(8,128)(2,1)}, u32[]{:S(2)}, u32[]{:S(2)}) async-start(bf16[128,192,128]{2,1,0:T(8,128)(2,1)} %copy.127), calls=%async_computation.3 | async-start | bytes 12582912 | tf_op jit(solution)/shard_map/all_to_all | solution.py:267
  444.8 0.7 reduce.4
  445.5 2.8 fusion.26
  448.3 1.3 copy.134
  449.7 73.7 %all-to-all-done.2 = bf16[128,192,128]{2,1,0:T(8,128)(2,1)} async-done(((bf16[128,192,128]{2,1,0:T(8,128)(2,1)}), bf16[128,192,128]{2,1,0:T(8,128)(2,1)}, u32[]{:S(2)}, u32[]{:S(2)}) %all-to-all-start.2) | async-done | bytes 6291488 | tf_op jit(solution)/shard_map/all_to_all | solution.py:267
  523.4 11.2 %gather_fusion.1 = bf16[1024,16,128]{2,1,0:T(8,128)(2,1)} fusion(bf16[1536,16,128]{2,1,0:T(8,128)(2,1)} %bitcast.50, s32[1024]{0:T(1024)S(1)} %broadcast_clamp_fusion), kind=kCustom, calls=%fused_computation.1 | custom fusion | bytes 8392704 | tf_op jit(solution)/shard_map/gather | solution.py:274
  534.5 3.5 fusion.6
  538.0 1.1 fusion.41
  (93 shorter events, 6.0 us)
Async XLA Ops:
  7.2 401.0 %copy-start = (bf16[1,768,2048]{2,1,0:T(8,128)(2,1)S(1)}, bf16[1,768,2048]{2,1,0:T(8,128)(2,1)}, u32[]{:S(2)}) copy-start(bf16[1,768,2048]{2,1,0:T(8,128)(2,1)} %param.35) | copy-start | bytes 9437188
  7.2 7.2 %copy-start.5 = (bf16[1,64,128]{2,1,0:T(8,128)(2,1)S(1)}, bf16[1,64,128]{2,1,0:T(8,128)(2,1)}, u32[]{:S(2)}) copy-start(bf16[1,64,128]{2,1,0:T(8,128)(2,1)} %param.28) | copy-start | bytes 49156
  7.2 7.3 %copy-start.6 = (bf16[1,64,128]{2,1,0:T(8,128)(2,1)S(1)}, bf16[1,64,128]{2,1,0:T(8,128)(2,1)}, u32[]{:S(2)}) copy-start(bf16[1,64,128]{2,1,0:T(8,128)(2,1)} %param.29) | copy-start | bytes 49156
  7.2 7.5 %copy-start.10 = (s32[1,8]{1,0:T(1,128)S(1)}, s32[1,8]{1,0:T(1,128)}, u32[]{:S(2)}) copy-start(s32[1,8]{1,0:T(1,128)} %param.31) | copy-start | bytes 100
  7.2 7.6 %copy-start.12 = (f32[128]{0:T(128)S(1)}, f32[128]{0:T(128)}, u32[]{:S(2)}) copy-start(f32[128]{0:T(128)} %param.25) | copy-start | bytes 1540
  18.4 74.5 %all-to-all-start = ((bf16[32,320,256]{2,1,0:T(8,128)(2,1)}), bf16[32,320,256]{2,1,0:T(8,128)(2,1)}, u32[]{:S(2)}, u32[]{:S(2)}) async-start(bf16[32,320,256]{2,1,0:T(8,128)(2,1)} %broadcast_in_dim.154), calls=%async_computation | async-start | bytes 10485760 | tf_op jit(solution)/shard_map/all_to_all | solution.py:191
  27.3 131.3 %reduce-scatter.2.cloned.1.call-start = ((), (), s32[]{:S(2)}) async-start(), calls=%async_computation.6 | async-start | bytes 1572864 | tf_op jit(solution)/shard_map/reduce_scatter | solution.py:229
  27.4 6.5 %copy-start.14 = (f32[2048]{0:T(1024)S(1)}, f32[2048]{0:T(1024)}, u32[]{:S(2)}) copy-start(f32[2048]{0:T(1024)} %param.20) | copy-start | bytes 24580
  33.9 4.2 copy-start.13
  42.2 53.2 %copy-start.3 = (s32[10240]{0:T(1024)}, s32[10240]{0:T(1024)S(1)}, u32[]{:S(2)}) copy-start(s32[10240]{0:T(1024)S(1)} %get-tuple-element.34) | copy-start | bytes 122884
  42.2 53.2 %copy-start.4 = (s32[10240]{0:T(1024)}, s32[10240]{0:T(1024)S(1)}, u32[]{:S(2)}) copy-start(s32[10240]{0:T(1024)S(1)} %get-tuple-element.35) | copy-start | bytes 122884
  127.8 4.6 copy-start.7
  132.4 28.4 %copy-start.9 = (f32[2048]{0:T(1024)S(1)}, f32[2048]{0:T(1024)}, u32[]{:S(2)}) copy-start(f32[2048]{0:T(1024)} %param.27) | copy-start | bytes 24580
  160.0 0.8 copy-start.1
  278.9 9.7 %copy-start.11 = (s32[8,1,2,1]{0,3,2,1:T(1,128)S(1)}, s32[8,1,2,1]{0,3,2,1:T(1,128)}, u32[]{:S(2)}) copy-start(s32[8,1,2,1]{0,3,2,1:T(1,128)} %param.37) | copy-start | bytes 196
  278.9 88.4 %all-to-all-start.1 = ((bf16[128,192,128]{2,1,0:T(8,128)(2,1)}), bf16[128,192,128]{2,1,0:T(8,128)(2,1)}, u32[]{:S(2)}, u32[]{:S(2)}) async-start(bf16[128,192,128]{2,1,0:T(8,128)(2,1)} %bitcast.175), calls=%async_computation.2 | async-start | bytes 12582912 | tf_op jit(solution)/shard_map/all_to_all | solution.py:265
  367.3 18.5 %all-to-all-start.3 = ((s32[1,32,1]{2,0,1:T(1,128)}), s32[1,32,1]{2,0,1:T(1,128)S(1)}, u32[]{:S(2)}, u32[]{:S(2)}) async-start(s32[1,32,1]{2,0,1:T(1,128)} %copy.131), calls=%async_computation.4 | async-start | bytes 32768 | tf_op jit(solution)/shard_map/all_to_all | solution.py:312
  385.9 47.0 %all-to-all-start.4 = ((bf16[1,32,128,256]{3,2,0,1:T(8,128)(2,1)}), bf16[1,32,128,256]{3,2,0,1:T(8,128)(2,1)}, u32[]{:S(2)}, u32[]{:S(2)}) async-start(bf16[1,32,128,256]{3,2,0,1:T(8,128)(2,1)} %bitcast.179), calls=%async_computation.5 | async-start | bytes 4194304 | tf_op jit(solution)/shard_map/all_to_all | solution.py:311
  432.8 11.8 %copy-start.8 = (f32[1,128,8]{1,2,0:T(8,128)S(1)}, f32[1,128,8]{1,2,0:T(8,128)}, u32[]{:S(2)}) copy-start(f32[1,128,8]{1,2,0:T(8,128)} %param.33) | copy-start | bytes 12292
  432.8 90.5 %all-to-all-start.2 = ((bf16[128,192,128]{2,1,0:T(8,128)(2,1)}), bf16[128,192,128]{2,1,0:T(8,128)(2,1)}, u32[]{:S(2)}, u32[]{:S(2)}) async-start(bf16[128,192,128]{2,1,0:T(8,128)(2,1)} %copy.127), calls=%async_computation.3 | async-start | bytes 12582912 | tf_op jit(solution)/shard_map/all_to_all | solution.py:267
  534.5 3.5 copy-start.2
Sparse Core Ops, SparseCore 0:
  132.6 25.9 reduce-scatter.1
